TPU v7x, 32 devices: a whole 2x2x4 slice. The times are simulated.
32 devices in a mesh: row: 16 (over z, y, x), col: 2 (over core).
Axes of the slice: x: 2, y: 2, z: 4, core: 2. Of those that a mesh axis runs over, the one named last changes fastest.
Arguments:
- air_state: bfloat16 [4096, 384], P(('row', 'col')), may hold values from -6 to 6
- owner_map: int32 [4096, 1], P(('row', 'col')), may hold values from 0 to 15; in each aligned block of 128 rows (0 to 127, 128 to 255, ...) at most 16 rows name the same one
- cost_class: int32 [4096], P(('row', 'col')), may hold values from 0 to 3
- connectivity: int32 [4, 4096], P(None, ('row', 'col')), may hold values from -32 to 32, as said below
- inverse_blocks: bfloat16 [32, 4, 3, 128, 128], P(('row', 'col')), may hold values from -0.5 to 0.5
Outputs:
- new_state: bfloat16 [4096, 384], P(('row', 'col'))
Inputs may be any that keep to these rules, and one draw needn't show every extreme that they name: `owner_map`: among the columns of one device no owner row is named by more than 16 columns, and some owner row is named by exactly 16. `connectivity`: offsets are never zero; both ends of the range occur.
All inputs are finite; a program needn't handle non-finite values.
Results may differ from a plain program's by a relative error of at most 0.0037.
Values may be sent and summed in bfloat16 or wider, within the bound.
No kernel may reach another device: no remote copies, remote signals or barrier semaphores. Data moves between devices by JAX's collectives and lax.ppermute only.
A program may use at most 128 MiB of HBM per device.

v0:
```python
import math

import jax
import jax.numpy as jnp
from jax import lax
from jax.sharding import PartitionSpec as P

viscosity = 0.25


def padded(cells, sides, width):
    for axis, dim in sides:
        count = lax.axis_size(axis)
        head = lax.slice_in_dim(cells, 0, width, axis=dim)
        tail = lax.slice_in_dim(cells, cells.shape[dim] - width, cells.shape[dim], axis=dim)
        cells = jnp.concatenate(
            [
                lax.ppermute(tail, axis, [(i, (i + 1) % count) for i in range(count)]),
                cells,
                lax.ppermute(head, axis, [((i + 1) % count, i) for i in range(count)]),
            ],
            axis=dim,
        )
    return cells


def apply_local(received, labels_in, inverse_blocks):
    layout_shape = received.shape
    levels = inverse_blocks.shape[-1]
    classes = inverse_blocks.shape[1]
    slot_total = layout_shape[0] * layout_shape[1]
    fields = received.reshape(slot_total, 3, levels)
    labels = labels_in.reshape(slot_total)
    block_rows = math.gcd(256, slot_total)
    class_values = jnp.arange(classes, dtype=jnp.int32).astype(jnp.bfloat16)
    own_blocks = inverse_blocks[0]

    def one_block(pair):
        field_block, label_block = pair
        selector = (label_block[:, None] == class_values[None, :]).astype(jnp.bfloat16)
        spread = field_block[:, None, :, :] * selector[:, :, None, None]
        result = jnp.einsum(
            "rcfm,cflm->rfl", spread, own_blocks, preferred_element_type=jnp.float32
        )
        return result.astype(jnp.bfloat16)

    computed = lax.map(
        one_block, (fields.reshape(-1, block_rows, 3, levels), labels.reshape(-1, block_rows))
    )
    return computed.reshape(layout_shape)


def pack_slots(air_state, targets, slot_index, cost_class, groups, capacity):
    outgoing = (
        jnp.zeros((groups, capacity, air_state.shape[1]), jnp.bfloat16)
        .at[targets, slot_index]
        .set(air_state)
    )
    labels_out = (
        jnp.full((groups, capacity), -1.0, jnp.bfloat16)
        .at[targets, slot_index]
        .set(cost_class.astype(jnp.bfloat16))
    )
    return (outgoing, labels_out)


def per_device(air_state, owner_map, cost_class, connectivity, inverse_blocks):
    groups = lax.axis_size("row")
    local_count = air_state.shape[0]
    capacity = 2 * local_count // groups
    targets = owner_map[:, 0]
    target_hits = (targets[:, None] == jnp.arange(groups, dtype=jnp.int32)[None, :]).astype(
        jnp.int32
    )
    slot_index = jnp.sum((jnp.cumsum(target_hits, axis=0) - 1) * target_hits, axis=1)
    halo_width = local_count // 4
    extended = padded(air_state, (("col", 0),), halo_width)
    center = air_state.astype(jnp.float32)
    places = jnp.arange(local_count, dtype=jnp.int32) + halo_width
    laplace_sum = jnp.zeros_like(center)
    for partner in range(connectivity.shape[0]):
        laplace_sum = laplace_sum + (
            extended[places + connectivity[partner]].astype(jnp.float32) - center
        )
    outgoing, labels_out = pack_slots(air_state, targets, slot_index, cost_class, groups, capacity)
    received, labels_in = (
        lax.all_to_all(outgoing, "row", split_axis=0, concat_axis=0, tiled=True),
        lax.all_to_all(labels_out, "row", split_axis=0, concat_axis=0, tiled=True),
    )
    computed = apply_local(received, labels_in, inverse_blocks)
    returned = lax.all_to_all(computed, "row", split_axis=0, concat_axis=0, tiled=True)
    physics = returned[targets, slot_index]
    return (physics.astype(jnp.float32) + viscosity * laplace_sum).astype(jnp.bfloat16)


def solution(mesh):
    return jax.shard_map(
        per_device,
        mesh=mesh,
        in_specs=(
            P(("row", "col"), None),
            P(("row", "col"), None),
            P(("row", "col")),
            P(None, ("row", "col")),
            P(("row", "col"), None, None, None, None),
        ),
        out_specs=P(("row", "col"), None),
        check_vma=False,
    )
```

profile of v0, /device:TPU:0, one launch (start us, length us, event | category | flops | bytes accessed | tf_op | source)
XLA Modules:
  0.0 66.7 jit_solution(6063689564514271344)
XLA Ops:
  0.0 0.8 %fusion.20 = (bf16[32,384]{1,0:T(8,128)(2,1)S(1)}, bf16[32,384]{1,0:T(8,128)(2,1)S(1)}) fusion(bf16[128,384]{1,0:T(8,128)(2,1)} %param.5), kind=kLoop, calls=%fused_computation.56 | loop fusion | bytes 98304 | tf_op jit(solution)/shard_map/slice | solution.py:14
  0.8 0.5 collective-permute-start
  1.3 0.1 collective-permute-start.1
  1.4 0.6 copy-done.2
  1.9 0.1 fusion.12
  2.0 0.2 reduce_window_sum.11
  2.2 0.2 select_reduce_fusion
  2.4 0.0 copy-start.4
  2.4 0.6 copy-done.4
  3.0 7.1 %scatter_fusion.1 = bf16[16,16]{1,0:T(8,128)(2,1)S(1)} fusion(bf16[16,16]{1,0:T(8,128)(2,1)S(1)} %broadcast_in_dim.11, s32[128]{0:T(128)S(1)} %get-tuple-element.15, bf16[128]{0:T(256)(128)(2,1)S(1)} %convert_element_type.50), kind=kCustom, calls=%fused_computation.6 | custom fusion | bytes 1792 | tf_op jit(solution)/shard_map/scatter | solution.py:62
  10.1 0.6 copy.15
  10.7 8.0 %all-to-all-start.1 = ((bf16[16,1,16]{2,1,0:T(2,128)(2,1)}), bf16[16,1,16]{2,1,0:T(2,128)(2,1)S(1)}, u32[]{:S(2)}, u32[]{:S(2)}) async-start(bf16[16,1,16]{2,1,0:T(2,128)(2,1)} %copy.15), calls=%async_computation.1 | async-start | bytes 16384 | tf_op jit(solution)/shard_map/all_to_all | solution.py:88
  18.8 0.0 copy-start.1
  18.8 0.7 %broadcast_in_dim.10 = bf16[16,16,384]{2,1,0:T(8,128)(2,1)} broadcast(bf16[]{:T(256)} %constant.9.clone.1), dimensions={} | broadcast | bytes 196610 | tf_op jit(solution)/shard_map/broadcast_in_dim | solution.py:55
  19.5 0.2 copy-done.1
  19.7 16.3 %scatter_fusion = bf16[16,16,384]{2,1,0:T(8,128)(2,1)} fusion(bf16[16,16,384]{2,1,0:T(8,128)(2,1)} %broadcast_in_dim.10, s32[128]{0:T(128)S(1)} %get-tuple-element.15, bf16[128,384]{1,0:T(8,128)(2,1)S(1)} %copy-done.1), kind=kCustom, calls=%fused_computation.5 | custom fusion | bytes 295936 | tf_op jit(solution)/shard_map/scatter | solution.py:57
  35.9 6.8 %all-to-all-start = ((bf16[16,16,384]{2,1,0:T(8,128)(2,1)}), bf16[16,16,384]{2,1,0:T(8,128)(2,1)S(1)}, u32[]{:S(2)}, u32[]{:S(2)}) async-start(bf16[16,16,384]{2,1,0:T(8,128)(2,1)} %scatter_fusion), calls=%async_computation | async-start | bytes 393216 | tf_op jit(solution)/shard_map/all_to_all | solution.py:87
  42.8 0.1 eq.45
  42.9 0.1 compare_convert_fusion
  43.0 8.6 %all-to-all-done = bf16[16,16,384]{2,1,0:T(8,128)(2,1)S(1)} async-done(((bf16[16,16,384]{2,1,0:T(8,128)(2,1)}), bf16[16,16,384]{2,1,0:T(8,128)(2,1)S(1)}, u32[]{:S(2)}, u32[]{:S(2)}) %all-to-all-start) | async-done | bytes 196640 | tf_op jit(solution)/shard_map/all_to_all | solution.py:87
  51.6 0.1 mul.32
  51.7 0.5 fusion.1
  52.2 0.2 copy.17
  52.4 0.8 %reshape.147 = bf16[16,16,384]{2,1,0:T(8,128)(2,1)} reshape(bf16[256,3,128]{2,1,0:T(4,128)(2,1)S(1)} %copy.17) | data formatting | bytes 393216 | tf_op jit(solution)/shard_map/reshape | solution.py:50
  53.2 3.5 %all-to-all-start.2 = ((bf16[16,16,384]{2,1,0:T(8,128)(2,1)}), bf16[16,16,384]{2,1,0:T(8,128)(2,1)S(1)}, u32[]{:S(2)}, u32[]{:S(2)}) async-start(bf16[16,16,384]{2,1,0:T(8,128)(2,1)} %reshape.147), calls=%async_computation.2 | async-start | bytes 393216 | tf_op jit(solution)/shard_map/all_to_all | solution.py:91
  56.8 0.9 %gather_fusion.1 = bf16[128,384]{1,0:T(8,128)(2,1)S(1)} fusion(bf16[192,384]{1,0:T(8,128)(2,1)S(1)} %constant_dynamic-update-slice_fusion, s32[1024]{0:T(1024)S(1)} %get-tuple-element.34), kind=kCustom, calls=%fused_computation.1 | custom fusion | bytes 197120 | tf_op jit(solution)/shard_map/gather | solution.py:83
  57.7 0.9 %gather_fusion.2 = bf16[128,384]{1,0:T(8,128)(2,1)S(1)} fusion(bf16[192,384]{1,0:T(8,128)(2,1)S(1)} %constant_dynamic-update-slice_fusion, s32[1024]{0:T(1024)S(1)} %get-tuple-element.33), kind=kCustom, calls=%fused_computation.2 | custom fusion | bytes 197120 | tf_op jit(solution)/shard_map/gather | solution.py:83
  58.5 0.9 %gather_fusion.3 = bf16[128,384]{1,0:T(8,128)(2,1)S(1)} fusion(bf16[192,384]{1,0:T(8,128)(2,1)S(1)} %constant_dynamic-update-slice_fusion, s32[1024]{0:T(1024)S(1)} %get-tuple-element.32), kind=kCustom, calls=%fused_computation.3 | custom fusion | bytes 197120 | tf_op jit(solution)/shard_map/gather | solution.py:83
  59.4 0.9 %gather_fusion.4 = bf16[128,384]{1,0:T(8,128)(2,1)S(1)} fusion(bf16[192,384]{1,0:T(8,128)(2,1)S(1)} %constant_dynamic-update-slice_fusion, s32[1024]{0:T(1024)S(1)} %get-tuple-element.31), kind=kCustom, calls=%fused_computation.4 | custom fusion | bytes 197120 | tf_op jit(solution)/shard_map/gather | solution.py:83
  60.3 4.5 %all-to-all-done.2 = bf16[16,16,384]{2,1,0:T(8,128)(2,1)S(1)} async-done(((bf16[16,16,384]{2,1,0:T(8,128)(2,1)}), bf16[16,16,384]{2,1,0:T(8,128)(2,1)S(1)}, u32[]{:S(2)}, u32[]{:S(2)}) %all-to-all-start.2) | async-done | bytes 196640 | tf_op jit(solution)/shard_map/all_to_all | solution.py:91
  64.8 1.2 %gather_fusion = bf16[128,384]{1,0:T(8,128)(2,1)S(1)} fusion(bf16[16,16,384]{2,1,0:T(8,128)(2,1)S(1)} %all-to-all-done.2, s32[128]{0:T(128)S(1)} %bitcast.50), kind=kCustom, calls=%fused_computation | custom fusion | bytes 197632 | tf_op jit(solution)/shard_map/gather | solution.py:92
  66.0 0.7 %fusion.11 = bf16[128,384]{1,0:T(8,128)(2,1)} fusion(bf16[128,384]{1,0:T(8,128)(2,1)S(1)} %copy-done.1, bf16[128,384]{1,0:T(8,128)(2,1)S(1)} %gather_fusion.4, bf16[128,384]{1,0:T(8,128)(2,1)S(1)} %gather_fusion.3, bf16[128,384]{1,0:T(8,128)(2,1)S(1)} %gather_fusion.2, bf16[128,384]{1,0:T(8,128)(2,1)S(1)} %gather_fusion.1, bf16[128,384]{1,0:T(8,128)(2,1)S(1)} %gather_fusion), kind=kLoop, calls=%fused_computation.23 | loop fusion | flops 786432 | bytes 688128 | tf_op jit(solution)/shard_map/convert_element_type | solution.py:93
  (20 shorter events, 0.2 us)
Async XLA Ops:
  0.0 51.7 %copy-start = (bf16[1,4,3,128,128]{4,3,2,1,0:T(8,128)(2,1)S(1)}, bf16[1,4,3,128,128]{4,3,2,1,0:T(8,128)(2,1)}, u32[]{:S(2)}) copy-start(bf16[1,4,3,128,128]{4,3,2,1,0:T(8,128)(2,1)} %param.9) | copy-start | bytes 1179652
  0.8 55.9 %collective-permute-start = (bf16[32,384]{1,0:T(8,128)(2,1)S(1)}, bf16[32,384]{1,0:T(8,128)(2,1)S(1)}, u32[]{:S(2)}, u32[]{:S(2)}) collective-permute-start(bf16[32,384]{1,0:T(8,128)(2,1)S(1)} %get-tuple-element.24), channel_id=1, source_target_pairs={{0,1},{1,0},{2,3},{3,2},{4,5},{5,4},{6,7},{7,6},{8,9},{9,8},{10,11... | collective-permute-start | bytes 73736 | tf_op jit(solution)/shard_map/ppermute | solution.py:18
  1.3 0.7 copy-start.2
  1.3 55.5 %collective-permute-start.1 = (bf16[32,384]{1,0:T(8,128)(2,1)S(1)}, bf16[32,384]{1,0:T(8,128)(2,1)S(1)}, u32[]{:S(2)}, u32[]{:S(2)}) collective-permute-start(bf16[32,384]{1,0:T(8,128)(2,1)S(1)} %get-tuple-element.17), channel_id=1, source_target_pairs={{1,0},{0,1},{3,2},{2,3},{5,4},{4,5},{7,6},{6,7},{9,8},{8,9},{11,10... | collective-permute-start | bytes 73736 | tf_op jit(solution)/shard_map/ppermute | solution.py:20
  2.4 0.7 copy-start.4
  10.7 8.0 %copy-start.3 = (s32[4,128]{1,0:T(4,128)S(1)}, s32[4,128]{1,0:T(4,128)}, u32[]{:S(2)}) copy-start(s32[4,128]{1,0:T(4,128)} %param.8) | copy-start | bytes 6148
  10.7 25.2 %all-to-all-start.1 = ((bf16[16,1,16]{2,1,0:T(2,128)(2,1)}), bf16[16,1,16]{2,1,0:T(2,128)(2,1)S(1)}, u32[]{:S(2)}, u32[]{:S(2)}) async-start(bf16[16,1,16]{2,1,0:T(2,128)(2,1)} %copy.15), calls=%async_computation.1 | async-start | bytes 16384 | tf_op jit(solution)/shard_map/all_to_all | solution.py:88
  18.8 0.9 %copy-start.1 = (bf16[128,384]{1,0:T(8,128)(2,1)S(1)}, bf16[128,384]{1,0:T(8,128)(2,1)}, u32[]{:S(2)}) copy-start(bf16[128,384]{1,0:T(8,128)(2,1)} %param.5) | copy-start | bytes 294916
  35.9 15.7 %all-to-all-start = ((bf16[16,16,384]{2,1,0:T(8,128)(2,1)}), bf16[16,16,384]{2,1,0:T(8,128)(2,1)S(1)}, u32[]{:S(2)}, u32[]{:S(2)}) async-start(bf16[16,16,384]{2,1,0:T(8,128)(2,1)} %scatter_fusion), calls=%async_computation | async-start | bytes 393216 | tf_op jit(solution)/shard_map/all_to_all | solution.py:87
  53.2 11.6 %all-to-all-start.2 = ((bf16[16,16,384]{2,1,0:T(8,128)(2,1)}), bf16[16,16,384]{2,1,0:T(8,128)(2,1)S(1)}, u32[]{:S(2)}, u32[]{:S(2)}) async-start(bf16[16,16,384]{2,1,0:T(8,128)(2,1)} %reshape.147), calls=%async_computation.2 | async-start | bytes 393216 | tf_op jit(solution)/shard_map/all_to_all | solution.py:91
where the time goes:
time: 67.5 us; the launch traced here: 66.7 us
  local copies, waits for them, and re-layouts  32.8 us (49%)
  starting transfers between devices  18.9 us (28%)
  waiting for transfers between devices  13.1 us (19%)
  other arithmetic  1.33 us (2%)
    scatter x1, local copies, waits for them, and re-layouts, pack_slots(): outgoing = jnp.zeros((groups, capacity, air_state.shape[1]), jnp.bfloat16...  16.3 us
    all_to_all x1, waiting for transfers between devices, per_device(): lax.all_to_all(outgoing, 'row', split_axis=0, concat_axis=0, tiled=True)  8.61 us
    all_to_all x1, starting transfers between devices, per_device(): lax.all_to_all(labels_out, 'row', split_axis=0, concat_axis=0, tiled=True)  8 us
    scatter x1, local copies, waits for them, and re-layouts, pack_slots(): labels_out = jnp.full((groups, capacity), -1.0, jnp.bfloat16).at[targets,...  7.09 us
    all_to_all x1, starting transfers between devices, per_device(): lax.all_to_all(outgoing, 'row', split_axis=0, concat_axis=0, tiled=True)  6.81 us
    all_to_all x1, waiting for transfers between devices, per_device(): lax.all_to_all(computed, 'row', split_axis=0, concat_axis=0, tiled=True)  4.49 us
    all_to_all x1, starting transfers between devices, per_device(): lax.all_to_all(computed, 'row', split_axis=0, concat_axis=0, tiled=True)  3.52 us
    gather x4, local copies, waits for them, and re-layouts, per_device(): extended[places + connectivity[partner]].astype(jnp.float32) - center  3.46 us
  transfers between devices with their start and end apart: 5, of which 2 were waited for; matrix products, arithmetic and copies ran while one was open for 46% of the time, Pallas kernels for 0%

commit v1 on v0

v1 whole, which is shorter than its diff:
```python
import jax
import jax.numpy as jnp
from jax import lax
from jax.sharding import PartitionSpec as P

viscosity = 0.25


def padded(cells, axis, width):
    count = lax.axis_size(axis)
    head = cells[:width]
    tail = cells[cells.shape[0] - width:]
    return jnp.concatenate(
        [
            lax.ppermute(tail, axis, [(i, (i + 1) % count) for i in range(count)]),
            cells,
            lax.ppermute(head, axis, [((i + 1) % count, i) for i in range(count)]),
        ],
        axis=0,
    )


def per_device(air_state, owner_map, cost_class, connectivity, inverse_blocks):
    groups = lax.axis_size("row")
    local_count, feat = air_state.shape
    levels = inverse_blocks.shape[-1]
    classes = inverse_blocks.shape[1]
    fields = feat // levels
    capacity = 2 * local_count // groups
    slots = groups * capacity

    targets = owner_map[:, 0]
    hits = (targets[:, None] == jnp.arange(groups, dtype=jnp.int32)[None, :]).astype(jnp.int32)
    slot_index = jnp.sum((jnp.cumsum(hits, axis=0) - 1) * hits, axis=1)
    dest = targets * capacity + slot_index
    pack = (jnp.arange(slots, dtype=jnp.int32)[:, None] == dest[None, :]).astype(jnp.bfloat16)

    label_lanes = jnp.broadcast_to(cost_class.astype(jnp.bfloat16)[:, None], (local_count, 128))
    air_ext = jnp.concatenate([air_state, label_lanes], axis=1)
    outgoing = jnp.dot(pack, air_ext, preferred_element_type=jnp.float32).astype(jnp.bfloat16)
    received = lax.all_to_all(
        outgoing.reshape(groups, capacity, feat + 128), "row", split_axis=0, concat_axis=0, tiled=True
    ).reshape(slots, feat + 128)

    halo = local_count // 4
    extended = padded(air_state, "col", halo)
    base = jnp.arange(local_count, dtype=jnp.int32)[:, None] + halo
    cols = jnp.arange(local_count + 2 * halo, dtype=jnp.int32)[None, :]
    counts = jnp.zeros((local_count, local_count + 2 * halo), jnp.float32)
    for partner in range(connectivity.shape[0]):
        counts = counts + (cols == base + connectivity[partner][:, None]).astype(jnp.float32)
    counts = counts - connectivity.shape[0] * (cols == base).astype(jnp.float32)
    band = (viscosity * counts).astype(jnp.bfloat16)
    lap = jnp.dot(band, extended, preferred_element_type=jnp.float32)

    labels = received[:, feat:feat + 1]
    own_blocks = inverse_blocks[0]
    outs = []
    for f in range(fields):
        xf = received[:, f * levels:(f + 1) * levels]
        acc = jnp.zeros((slots, levels), jnp.float32)
        for c in range(classes):
            r = lax.dot_general(
                xf, own_blocks[c, f], (((1,), (1,)), ((), ())), preferred_element_type=jnp.float32
            )
            acc = jnp.where(labels == c, r, acc)
        outs.append(acc.astype(jnp.bfloat16))
    computed = jnp.concatenate(outs, axis=1)
    returned = lax.all_to_all(
        computed.reshape(groups, capacity, feat), "row", split_axis=0, concat_axis=0, tiled=True
    ).reshape(slots, feat)
    physics = lax.dot_general(
        pack, returned, (((0,), (0,)), ((), ())), preferred_element_type=jnp.float32
    )
    return (physics + lap).astype(jnp.bfloat16)


def solution(mesh):
    return jax.shard_map(
        per_device,
        mesh=mesh,
        in_specs=(
            P(("row", "col"), None),
            P(("row", "col"), None),
            P(("row", "col")),
            P(None, ("row", "col")),
            P(("row", "col"), None, None, None, None),
        ),
        out_specs=P(("row", "col"), None),
        check_vma=False,
    )
```

time: 67.5 us -> 36.4 us (0.54)
  local copies, waits for them, and re-layouts: 32.8 us -> 2.31 us
  blocking collectives: 0 us -> 18 us
  starting transfers between devices: 18.9 us -> 4.11 us
  waiting for transfers between devices: 13.1 us -> 7.38 us
  matrix products: 0.46 us -> 3.36 us
    scatter x2 -> x0, local copies, waits for them, and re-layouts: 23.4 us -> none  [the longest x1 16.3 us: pack_slots(): outgoing = jnp.zeros((groups, capacity, air_state.shape[1]), jnp.bfloat16...]
    all_to_all x0 -> x1, blocking collectives: none -> 18 us  [per_device(): lax.all_to_all(outgoing.reshape(groups, capacity, feat + 128), 'row', spl...]
    all_to_all x3 -> x1, starting transfers between devices: 18.3 us -> 3.54 us  [per_device(): lax.all_to_all(computed.reshape(groups, capacity, feat), 'row', split_axi...]
    all_to_all x3 -> x1, waiting for transfers between devices: 13.1 us -> 7.37 us  [per_device(): lax.all_to_all(computed.reshape(groups, capacity, feat), 'row', split_axi...]
    gather x5 -> x0, local copies, waits for them, and re-layouts: 4.69 us -> none  [the longest x4 3.46 us: per_device(): extended[places + connectivity[partner]].astype(jnp.float32) - center]
    dot_general x1 -> x15, matrix products: 0.46 us -> 3.36 us  [the longest x12 1.99 us: per_device(): lax.dot_general(xf, own_blocks[c, f], (((1,), (1,)), ((), ())), preferred...]
    reshape x1 -> x0, local copies, waits for them, and re-layouts: 0.84 us -> none  [apply_local(): return computed.reshape(layout_shape)]
    convert_element_type x4 -> x1, other arithmetic: 0.84 us -> 0.01 us  [per_device(): cost_class.astype(jnp.bfloat16)[:, None]]
  transfers between devices with their start and end apart: 5 -> 3, of which waited for: 2 -> 1; matrix products, arithmetic and copies ran while one was open for 46% -> 1% of each run, Pallas kernels for 0% -> 0%
where the time goes in v1:
time: 36.4 us; the launch traced here: 36.1 us
  blocking collectives  18 us (49%)
  waiting for transfers between devices  7.38 us (20%)
  starting transfers between devices  4.11 us (11%)
  matrix products  3.36 us (9%)
  local copies, waits for them, and re-layouts  2.31 us (6%)
  other arithmetic  0.68 us (2%)
    all_to_all x1, blocking collectives, per_device(): lax.all_to_all(outgoing.reshape(groups, capacity, feat + 128), 'row', spl...  18 us
    all_to_all x1, waiting for transfers between devices, per_device(): lax.all_to_all(computed.reshape(groups, capacity, feat), 'row', split_axi...  7.37 us
    all_to_all x1, starting transfers between devices, per_device(): lax.all_to_all(computed.reshape(groups, capacity, feat), 'row', split_axi...  3.54 us
    dot_general x12, matrix products, per_device(): lax.dot_general(xf, own_blocks[c, f], (((1,), (1,)), ((), ())), preferred...  1.99 us
    unnamed x10, local copies, waits for them, and re-layouts  1.41 us
    dot_general x1, matrix products, per_device(): lap = jnp.dot(band, extended, preferred_element_type=jnp.float32)  0.93 us
    concatenate x1, local copies, waits for them, and re-layouts, per_device(): computed = jnp.concatenate(outs, axis=1)  0.81 us
  transfers between devices with their start and end apart: 3, of which 1 were waited for; matrix products, arithmetic and copies ran while one was open for 1% of the time, Pallas kernels for 0%

profile of v1, /device:TPU:0, one launch (start us, length us, event | category | flops | bytes accessed | tf_op | source)
XLA Modules:
  0.0 36.1 jit_solution(16274648755108814053)
XLA Ops:
  0.0 0.7 %copy-done.2 = s32[128,1]{0,1:T(1,128)S(1)} copy-done((s32[128,1]{0,1:T(1,128)S(1)}, s32[128,1]{0,1:T(1,128)}, u32[]{:S(2)}) %copy-start.2) | copy-done | bytes 536
  0.7 0.1 fusion.32
  0.7 0.0 copy-start.1
  0.8 0.2 reduce_window_sum.11
  0.9 0.2 select_reduce_fusion
  1.1 0.0 copy-start.4
  1.1 0.6 %copy-done.4 = s32[128]{0:T(128)S(1)} copy-done((s32[128]{0:T(128)S(1)}, s32[128]{0:T(128)}, u32[]{:S(2)}) %copy-start.4) | copy-done | bytes 536
  1.8 0.1 broadcast_in_dim.66
  1.9 0.2 convolution_convert_fusion
  2.1 18.0 %all_to_all.10 = bf16[16,16,512]{2,1,0:T(8,128)(2,1)S(1)} all-to-all(bf16[16,16,512]{2,1,0:T(8,128)(2,1)S(1)} %bitcast.65), channel_id=1, replica_groups=mesh['row'=16,'col'=2] {'row'}, dimensions={0} | all-to-all | bytes 524288 | tf_op jit(solution)/shard_map/all_to_all | solution.py:41
  20.1 0.2 fusion.48
  20.3 0.2 fusion.50
  20.4 0.2 fusion.52
  20.6 0.2 compare_reduce_fusion.3
  20.8 0.2 fusion.41
  21.0 0.2 fusion.43
  21.2 0.2 fusion.45
  21.3 0.2 fusion.34
  21.5 0.2 fusion.36
  21.7 0.2 fusion.38
  21.8 0.2 fusion.10
  22.0 0.2 fusion.11
  22.2 0.2 fusion.12
  22.4 0.8 %copy.8 = bf16[256,384]{1,0:T(8,128)(2,1)} copy(bf16[256,384]{0,1:T(8,128)(2,1)S(1)} %pad_maximum_fusion) | data formatting | bytes 393216 | tf_op jit(solution)/shard_map/concatenate | solution.py:68
  23.2 3.5 %all-to-all-start.1 = ((bf16[16,16,384]{2,1,0:T(8,128)(2,1)}), bf16[16,16,384]{2,1,0:T(8,128)(2,1)S(1)}, u32[]{:S(2)}, u32[]{:S(2)}) async-start(bf16[16,16,384]{2,1,0:T(8,128)(2,1)} %bitcast.16), calls=%async_computation.1 | async-start | bytes 393216 | tf_op jit(solution)/shard_map/all_to_all | solution.py:69
  26.8 0.0 copy-start.3
  26.8 0.1 collective-permute-start
  26.9 0.5 %collective-permute-start.1 = (bf16[32,384]{1,0:T(8,128)(2,1)S(1)}, bf16[32,384]{1,0:T(8,128)(2,1)S(1)}, u32[]{:S(2)}, u32[]{:S(2)}) collective-permute-start(bf16[32,384]{1,0:T(8,128)(2,1)S(1)} %get-tuple-element.10), channel_id=1, source_target_pairs={{1,0},{0,1},{3,2},{2,3},{5,4},{4,5},{7,6},{6,7},{9,8},{8,9},{11,10... | collective-permute-start | bytes 73736 | tf_op jit(solution)/shard_map/ppermute | solution.py:17
  27.4 0.1 copy-done.3
  27.5 7.4 %all-to-all-done.1 = bf16[16,16,384]{2,1,0:T(8,128)(2,1)S(1)} async-done(((bf16[16,16,384]{2,1,0:T(8,128)(2,1)}), bf16[16,16,384]{2,1,0:T(8,128)(2,1)S(1)}, u32[]{:S(2)}, u32[]{:S(2)}) %all-to-all-start.1) | async-done | bytes 196640 | tf_op jit(solution)/shard_map/all_to_all | solution.py:69
  34.9 0.2 fusion.21
  35.1 0.9 %fusion = bf16[128,384]{1,0:T(8,128)(2,1)} fusion(f32[128,384]{1,0:T(8,128)S(1)} %fusion.21, bf16[32,384]{1,0:T(8,128)(2,1)S(1)} %collective-permute-done.1, bf16[128,384]{1,0:T(8,128)(2,1)S(1)} %copy-done.1, bf16[32,384]{1,0:T(8,128)(2,1)S(1)} %collective-permute-done, s32[128]{0:T(128)S(1)} %get-tuple-element.15, s32[128]{0:T(128)S(1)} %get-tuple-element.13, ...), kind=kOutput, calls=%fused_computation.2 | convolution fusion | flops 19808256 | bytes 444928 | tf_op jit(solution)/shard_map/dot_general | solution.py:54
  (11 shorter events, 0.1 us)
Async XLA Ops:
  0.0 0.7 %copy-start.2 = (s32[128,1]{0,1:T(1,128)S(1)}, s32[128,1]{0,1:T(1,128)}, u32[]{:S(2)}) copy-start(s32[128,1]{0,1:T(1,128)} %param.6) | copy-start | bytes 1540
  0.7 1.1 %copy-start.1 = (bf16[128,384]{1,0:T(8,128)(2,1)S(1)}, bf16[128,384]{1,0:T(8,128)(2,1)}, u32[]{:S(2)}) copy-start(bf16[128,384]{1,0:T(8,128)(2,1)} %param.5) | copy-start | bytes 294916
  1.1 0.7 %copy-start.4 = (s32[128]{0:T(128)S(1)}, s32[128]{0:T(128)}, u32[]{:S(2)}) copy-start(s32[128]{0:T(128)} %param.7) | copy-start | bytes 1540
  1.9 18.2 %copy-start = (bf16[1,4,3,128,128]{4,3,2,1,0:T(8,128)(2,1)S(1)}, bf16[1,4,3,128,128]{4,3,2,1,0:T(8,128)(2,1)}, u32[]{:S(2)}) copy-start(bf16[1,4,3,128,128]{4,3,2,1,0:T(8,128)(2,1)} %param.9) | copy-start | bytes 1179652
  23.2 11.6 %all-to-all-start.1 = ((bf16[16,16,384]{2,1,0:T(8,128)(2,1)}), bf16[16,16,384]{2,1,0:T(8,128)(2,1)S(1)}, u32[]{:S(2)}, u32[]{:S(2)}) async-start(bf16[16,16,384]{2,1,0:T(8,128)(2,1)} %bitcast.16), calls=%async_computation.1 | async-start | bytes 393216 | tf_op jit(solution)/shard_map/all_to_all | solution.py:69
  26.8 0.7 %copy-start.3 = (s32[4,128]{1,0:T(4,128)S(1)}, s32[4,128]{1,0:T(4,128)}, u32[]{:S(2)}) copy-start(s32[4,128]{1,0:T(4,128)} %param.8) | copy-start | bytes 6148
  26.8 8.3 %collective-permute-start = (bf16[32,384]{1,0:T(8,128)(2,1)S(1)}, bf16[32,384]{1,0:T(8,128)(2,1)S(1)}, u32[]{:S(2)}, u32[]{:S(2)}) collective-permute-start(bf16[32,384]{1,0:T(8,128)(2,1)S(1)} %get-tuple-element.9), channel_id=1, source_target_pairs={{0,1},{1,0},{2,3},{3,2},{4,5},{5,4},{6,7},{7,6},{8,9},{9,8},{10,11... | collective-permute-start | bytes 73736 | tf_op jit(solution)/shard_map/ppermute | solution.py:15
  26.9 8.2 %collective-permute-start.1 = (bf16[32,384]{1,0:T(8,128)(2,1)S(1)}, bf16[32,384]{1,0:T(8,128)(2,1)S(1)}, u32[]{:S(2)}, u32[]{:S(2)}) collective-permute-start(bf16[32,384]{1,0:T(8,128)(2,1)S(1)} %get-tuple-element.10), channel_id=1, source_target_pairs={{1,0},{0,1},{3,2},{2,3},{5,4},{4,5},{7,6},{6,7},{9,8},{8,9},{11,10... | collective-permute-start | bytes 73736 | tf_op jit(solution)/shard_map/ppermute | solution.py:17

commit v2 on v1

--- a/solution.py
+++ b/solution.py
@@ -1,6 +1,8 @@
 import jax
 import jax.numpy as jnp
 from jax import lax
+from jax.experimental import pallas as pl
+from jax.experimental.pallas import tpu as pltpu
 from jax.sharding import PartitionSpec as P
 
 viscosity = 0.25
@@ -18,6 +20,37 @@
         ],
         axis=0,
     )
+
+
+def owner_kernel(x_ref, m_ref, o_ref):
+    classes, fields, levels = m_ref.shape[0], m_ref.shape[1], m_ref.shape[2]
+    feat = fields * levels
+    labels = x_ref[:, feat:feat + 1].astype(jnp.float32)
+    for f in range(fields):
+        xf = x_ref[:, f * levels:(f + 1) * levels]
+        acc = None
+        for c in range(classes):
+            r = lax.dot_general(
+                xf, m_ref[c, f], (((1,), (1,)), ((), ())), preferred_element_type=jnp.float32
+            )
+            acc = r if acc is None else jnp.where(labels == c, r, acc)
+        o_ref[:, f * levels:(f + 1) * levels] = acc.astype(o_ref.dtype)
+
+
+def apply_owner(received, own_blocks):
+    slots = received.shape[0]
+    classes, fields, levels = own_blocks.shape[0], own_blocks.shape[1], own_blocks.shape[2]
+    return pl.pallas_call(
+        owner_kernel,
+        out_shape=jax.ShapeDtypeStruct((slots, fields * levels), jnp.bfloat16),
+        in_specs=[pl.BlockSpec(memory_space=pltpu.VMEM)] * 2,
+        out_specs=pl.BlockSpec(memory_space=pltpu.VMEM),
+        cost_estimate=pl.CostEstimate(
+            flops=2 * slots * classes * fields * levels * levels,
+            transcendentals=0,
+            bytes_accessed=2 * (received.size + own_blocks.size + slots * fields * levels),
+        ),
+    )(received, own_blocks)
 
 
 def per_device(air_state, owner_map, cost_class, connectivity, inverse_blocks):
@@ -53,19 +86,7 @@
     band = (viscosity * counts).astype(jnp.bfloat16)
     lap = jnp.dot(band, extended, preferred_element_type=jnp.float32)
 
-    labels = received[:, feat:feat + 1]
-    own_blocks = inverse_blocks[0]
-    outs = []
-    for f in range(fields):
-        xf = received[:, f * levels:(f + 1) * levels]
-        acc = jnp.zeros((slots, levels), jnp.float32)
-        for c in range(classes):
-            r = lax.dot_general(
-                xf, own_blocks[c, f], (((1,), (1,)), ((), ())), preferred_element_type=jnp.float32
-            )
-            acc = jnp.where(labels == c, r, acc)
-        outs.append(acc.astype(jnp.bfloat16))
-    computed = jnp.concatenate(outs, axis=1)
+    computed = apply_owner(received, inverse_blocks[0])
     returned = lax.all_to_all(
         computed.reshape(groups, capacity, feat), "row", split_axis=0, concat_axis=0, tiled=True
     ).reshape(slots, feat)

time: 36.4 us -> 35.5 us (0.975)
  Pallas kernels: 0 us -> 2.12 us
  matrix products: 3.36 us -> 1.37 us
  local copies, waits for them, and re-layouts: 2.31 us -> 1.5 us
    pallas_call x0 -> x1, Pallas kernels: none -> 2.12 us  [apply_owner(): pl.pallas_call(owner_kernel, out_shape=jax.ShapeDtypeStruct((slots, field...]
    dot_general x12 -> x0, matrix products: 1.99 us -> none  [per_device(): lax.dot_general(xf, own_blocks[c, f], (((1,), (1,)), ((), ())), preferred...]
    concatenate x1 -> x0, local copies, waits for them, and re-layouts: 0.81 us -> none  [per_device(): computed = jnp.concatenate(outs, axis=1)]
    unnamed x10 -> x8, local copies, waits for them, and re-layouts: 1.41 us -> 1.41 us
where the time goes in v2:
time: 35.5 us; the launch traced here: 35.1 us
  blocking collectives  18.1 us (51%)
  waiting for transfers between devices  7.38 us (21%)
  starting transfers between devices  4.11 us (12%)
  Pallas kernels  2.12 us (6%)
  local copies, waits for them, and re-layouts  1.5 us (4%)
  matrix products  1.37 us (4%)
  other arithmetic  0.44 us (1%)
    all_to_all x1, blocking collectives, per_device(): lax.all_to_all(outgoing.reshape(groups, capacity, feat + 128), 'row', spl...  18.1 us
    all_to_all x1, waiting for transfers between devices, per_device(): lax.all_to_all(computed.reshape(groups, capacity, feat), 'row', split_axi...  7.37 us
    all_to_all x1, starting transfers between devices, per_device(): lax.all_to_all(computed.reshape(groups, capacity, feat), 'row', split_axi...  3.54 us
    pallas_call x1, Pallas kernels, apply_owner(): pl.pallas_call(owner_kernel, out_shape=jax.ShapeDtypeStruct((slots, field...  2.12 us
    unnamed x8, local copies, waits for them, and re-layouts  1.41 us
    dot_general x1, matrix products, per_device(): lap = jnp.dot(band, extended, preferred_element_type=jnp.float32)  0.93 us
  transfers between devices with their start and end apart: 3, of which 1 were waited for; matrix products, arithmetic and copies ran while one was open for 1% of the time, Pallas kernels for 0%

profile of v2, /device:TPU:0, one launch (start us, length us, event | category | flops | bytes accessed | tf_op | source)
XLA Modules:
  0.0 35.1 jit_solution(17749274762359069301)
XLA Ops:
  0.0 0.0 copy-start.1
  0.0 0.7 %copy-done.1 = s32[128,1]{0,1:T(1,128)S(1)} copy-done((s32[128,1]{0,1:T(1,128)S(1)}, s32[128,1]{0,1:T(1,128)}, u32[]{:S(2)}) %copy-start.1) | copy-done | bytes 536
  0.7 0.1 fusion.20
  0.7 0.0 copy-start
  0.8 0.2 reduce_window_sum.11
  0.9 0.2 select_reduce_fusion
  1.1 0.0 copy-start.3
  1.1 0.6 %copy-done.3 = s32[128]{0:T(128)S(1)} copy-done((s32[128]{0:T(128)S(1)}, s32[128]{0:T(128)}, u32[]{:S(2)}) %copy-start.3) | copy-done | bytes 536
  1.8 0.1 broadcast_in_dim.2
  1.9 0.0 copy-done
  1.9 0.2 convolution_convert_fusion
  2.1 18.1 %all_to_all.10 = bf16[16,16,512]{2,1,0:T(8,128)(2,1)} all-to-all(bf16[16,16,512]{2,1,0:T(8,128)(2,1)S(1)} %bitcast.16), channel_id=1, replica_groups=mesh['row'=16,'col'=2] {'row'}, dimensions={0} | all-to-all | bytes 524288 | tf_op jit(solution)/shard_map/all_to_all | solution.py:74
  20.2 2.1 %shard_map.55 = bf16[256,384]{1,0:T(8,128)(2,1)} custom-call(bf16[256,512]{1,0:T(8,128)(2,1)} %bitcast.17, bf16[4,3,128,128]{3,2,1,0:T(8,128)(2,1)} %bitcast.20), custom_call_target="tpu_custom_call" | custom-call | flops 100663296 | bytes 851968 | tf_op jit(solution)/shard_map/pallas_call | solution.py:43
  22.3 3.5 %all-to-all-start.1 = ((bf16[16,16,384]{2,1,0:T(8,128)(2,1)}), bf16[16,16,384]{2,1,0:T(8,128)(2,1)S(1)}, u32[]{:S(2)}, u32[]{:S(2)}) async-start(bf16[16,16,384]{2,1,0:T(8,128)(2,1)} %bitcast.19), calls=%async_computation.1 | async-start | bytes 393216 | tf_op jit(solution)/shard_map/all_to_all | solution.py:90
  25.9 0.0 copy-start.2
  25.9 0.1 collective-permute-start
  26.0 0.5 %collective-permute-start.1 = (bf16[32,384]{1,0:T(8,128)(2,1)S(1)}, bf16[32,384]{1,0:T(8,128)(2,1)S(1)}, u32[]{:S(2)}, u32[]{:S(2)}) collective-permute-start(bf16[32,384]{1,0:T(8,128)(2,1)S(1)} %get-tuple-element.6), channel_id=1, source_target_pairs={{1,0},{0,1},{3,2},{2,3},{5,4},{4,5},{7,6},{6,7},{9,8},{8,9},{11,10... | collective-permute-start | bytes 73736 | tf_op jit(solution)/shard_map/ppermute | solution.py:19
  26.5 0.1 copy-done.2
  26.6 7.4 %all-to-all-done.1 = bf16[16,16,384]{2,1,0:T(8,128)(2,1)S(1)} async-done(((bf16[16,16,384]{2,1,0:T(8,128)(2,1)}), bf16[16,16,384]{2,1,0:T(8,128)(2,1)S(1)}, u32[]{:S(2)}, u32[]{:S(2)}) %all-to-all-start.1) | async-done | bytes 196640 | tf_op jit(solution)/shard_map/all_to_all | solution.py:90
  33.9 0.2 fusion.9
  34.2 0.0 collective-permute-done
  34.2 0.0 collective-permute-done.1
  34.2 0.9 %fusion = bf16[128,384]{1,0:T(8,128)(2,1)} fusion(f32[128,384]{1,0:T(8,128)S(1)} %fusion.9, bf16[32,384]{1,0:T(8,128)(2,1)S(1)} %collective-permute-done.1, bf16[128,384]{1,0:T(8,128)(2,1)S(1)} %copy-done, bf16[32,384]{1,0:T(8,128)(2,1)S(1)} %collective-permute-done, s32[128]{0:T(128)S(1)} %get-tuple-element.11, s32[128]{0:T(128)S(1)} %get-tuple-element.9, ...), kind=kOutput, calls=%fused_computation.2 | convolution fusion | flops 19808256 | bytes 444928 | tf_op jit(solution)/shard_map/dot_general | solution.py:87
  (4 shorter events, 0.0 us)
Async XLA Ops:
  0.0 0.7 %copy-start.1 = (s32[128,1]{0,1:T(1,128)S(1)}, s32[128,1]{0,1:T(1,128)}, u32[]{:S(2)}) copy-start(s32[128,1]{0,1:T(1,128)} %param.6) | copy-start | bytes 1540
  0.7 1.1 %copy-start = (bf16[128,384]{1,0:T(8,128)(2,1)S(1)}, bf16[128,384]{1,0:T(8,128)(2,1)}, u32[]{:S(2)}) copy-start(bf16[128,384]{1,0:T(8,128)(2,1)} %param.5) | copy-start | bytes 294916
  1.1 0.7 %copy-start.3 = (s32[128]{0:T(128)S(1)}, s32[128]{0:T(128)}, u32[]{:S(2)}) copy-start(s32[128]{0:T(128)} %param.7) | copy-start | bytes 1540
  22.3 11.6 %all-to-all-start.1 = ((bf16[16,16,384]{2,1,0:T(8,128)(2,1)}), bf16[16,16,384]{2,1,0:T(8,128)(2,1)S(1)}, u32[]{:S(2)}, u32[]{:S(2)}) async-start(bf16[16,16,384]{2,1,0:T(8,128)(2,1)} %bitcast.19), calls=%async_computation.1 | async-start | bytes 393216 | tf_op jit(solution)/shard_map/all_to_all | solution.py:90
  25.9 0.7 %copy-start.2 = (s32[4,128]{1,0:T(4,128)S(1)}, s32[4,128]{1,0:T(4,128)}, u32[]{:S(2)}) copy-start(s32[4,128]{1,0:T(4,128)} %param.8) | copy-start | bytes 6148
  25.9 8.3 %collective-permute-start = (bf16[32,384]{1,0:T(8,128)(2,1)S(1)}, bf16[32,384]{1,0:T(8,128)(2,1)S(1)}, u32[]{:S(2)}, u32[]{:S(2)}) collective-permute-start(bf16[32,384]{1,0:T(8,128)(2,1)S(1)} %get-tuple-element.5), channel_id=1, source_target_pairs={{0,1},{1,0},{2,3},{3,2},{4,5},{5,4},{6,7},{7,6},{8,9},{9,8},{10,11... | collective-permute-start | bytes 73736 | tf_op jit(solution)/shard_map/ppermute | solution.py:17
  26.0 8.2 %collective-permute-start.1 = (bf16[32,384]{1,0:T(8,128)(2,1)S(1)}, bf16[32,384]{1,0:T(8,128)(2,1)S(1)}, u32[]{:S(2)}, u32[]{:S(2)}) collective-permute-start(bf16[32,384]{1,0:T(8,128)(2,1)S(1)} %get-tuple-element.6), channel_id=1, source_target_pairs={{1,0},{0,1},{3,2},{2,3},{5,4},{4,5},{7,6},{6,7},{9,8},{8,9},{11,10... | collective-permute-start | bytes 73736 | tf_op jit(solution)/shard_map/ppermute | solution.py:19

commit v3 on v2

--- a/solution.py
+++ b/solution.py
@@ -22,19 +22,37 @@
     )
 
 
-def owner_kernel(x_ref, m_ref, o_ref):
-    classes, fields, levels = m_ref.shape[0], m_ref.shape[1], m_ref.shape[2]
+def owner_kernel(x_hbm, m_hbm, o_hbm, xbuf, mbuf, obuf, sems):
+    classes, fields, levels = mbuf.shape[0], mbuf.shape[1], mbuf.shape[2]
     feat = fields * levels
-    labels = x_ref[:, feat:feat + 1].astype(jnp.float32)
+    fetch_x = pltpu.make_async_copy(x_hbm, xbuf, sems.at[0])
+    fetch_x.start()
+    fetch_m = [
+        pltpu.make_async_copy(m_hbm.at[:, f], mbuf.at[:, f], sems.at[1 + f]) for f in range(fields)
+    ]
+    for copy in fetch_m:
+        copy.start()
+    fetch_x.wait()
+    labels = xbuf[:, feat:feat + 1].astype(jnp.float32)
+    stores = []
     for f in range(fields):
-        xf = x_ref[:, f * levels:(f + 1) * levels]
-        acc = None
-        for c in range(classes):
-            r = lax.dot_general(
-                xf, m_ref[c, f], (((1,), (1,)), ((), ())), preferred_element_type=jnp.float32
-            )
-            acc = r if acc is None else jnp.where(labels == c, r, acc)
-        o_ref[:, f * levels:(f + 1) * levels] = acc.astype(o_ref.dtype)
+        fetch_m[f].wait()
+        xf = xbuf[:, f * levels:(f + 1) * levels]
+        stacked = mbuf[:, f].reshape(classes * levels, levels)
+        r = lax.dot_general(xf, stacked, (((1,), (1,)), ((), ())), preferred_element_type=jnp.float32)
+        acc = r[:, :levels]
+        for c in range(1, classes):
+            acc = jnp.where(labels == c, r[:, c * levels:(c + 1) * levels], acc)
+        obuf[:, f * levels:(f + 1) * levels] = acc.astype(obuf.dtype)
+        store = pltpu.make_async_copy(
+            obuf.at[:, pl.ds(f * levels, levels)],
+            o_hbm.at[:, pl.ds(f * levels, levels)],
+            sems.at[1 + fields + f],
+        )
+        store.start()
+        stores.append(store)
+    for store in stores:
+        store.wait()
 
 
 def apply_owner(received, own_blocks):
@@ -43,8 +61,14 @@
     return pl.pallas_call(
         owner_kernel,
         out_shape=jax.ShapeDtypeStruct((slots, fields * levels), jnp.bfloat16),
-        in_specs=[pl.BlockSpec(memory_space=pltpu.VMEM)] * 2,
-        out_specs=pl.BlockSpec(memory_space=pltpu.VMEM),
+        in_specs=[pl.BlockSpec(memory_space=pl.ANY)] * 2,
+        out_specs=pl.BlockSpec(memory_space=pl.ANY),
+        scratch_shapes=[
+            pltpu.VMEM(received.shape, received.dtype),
+            pltpu.VMEM(own_blocks.shape, own_blocks.dtype),
+            pltpu.VMEM((slots, fields * levels), jnp.bfloat16),
+            pltpu.SemaphoreType.DMA((1 + 2 * fields,)),
+        ],
         cost_estimate=pl.CostEstimate(
             flops=2 * slots * classes * fields * levels * levels,
             transcendentals=0,
@@ -86,6 +110,7 @@
     band = (viscosity * counts).astype(jnp.bfloat16)
     lap = jnp.dot(band, extended, preferred_element_type=jnp.float32)
 
+    received, lap = lax.optimization_barrier((received, lap))
     computed = apply_owner(received, inverse_blocks[0])
     returned = lax.all_to_all(
         computed.reshape(groups, capacity, feat), "row", split_axis=0, concat_axis=0, tiled=True

time: 35.5 us -> 37.4 us (1.054)
  blocking collectives: 18.1 us -> 11.6 us
  starting transfers between devices: 4.11 us -> 8.88 us
  waiting for transfers between devices: 7.38 us -> 8.88 us
  matrix products: 1.37 us -> 2.06 us
  other arithmetic: 0.44 us -> 1.09 us
  local copies, waits for them, and re-layouts: 1.5 us -> 1.97 us
    all_to_all x1, blocking collectives: 18.1 us -> 11.6 us  [per_device(): lax.all_to_all(computed.reshape(groups, capacity, feat), 'row', split_axi...]
    all_to_all x1, starting transfers between devices: 3.54 us -> 8.31 us  [per_device(): lax.all_to_all(outgoing.reshape(groups, capacity, feat + 128), 'row', spl...]
    all_to_all x1, waiting for transfers between devices: 7.37 us -> 8.14 us  [per_device(): lax.all_to_all(outgoing.reshape(groups, capacity, feat + 128), 'row', spl...]
    dot_general x1, matrix products: 0.22 us -> 0.91 us  [per_device(): jnp.dot(pack, air_ext, preferred_element_type=jnp.float32)]
    convert_element_type x1, other arithmetic: 0.01 us -> 0.66 us  [per_device(): cost_class.astype(jnp.bfloat16)[:, None]]
    dot_general x1, matrix products: 0.93 us -> 0.28 us  [per_device(): lap = jnp.dot(band, extended, preferred_element_type=jnp.float32)]
    dot_general x1, matrix products: 0.23 us -> 0.87 us  [per_device(): lax.dot_general(pack, returned, (((0,), (0,)), ((), ())), preferred_eleme...]
    ppermute x1, waiting for transfers between devices: 0.01 us -> 0.58 us  [padded(): lax.ppermute(head, axis, [((i + 1) % count, i) for i in range(count)])]
  transfers between devices with their start and end apart: 3 -> 3, of which waited for: 1 -> 3; matrix products, arithmetic and copies ran while one was open for 1% -> 1% of each run, Pallas kernels for 0% -> 0%
where the time goes in v3:
time: 37.4 us; the launch traced here: 37 us
  blocking collectives  11.6 us (31%)
  starting transfers between devices  8.88 us (24%)
  waiting for transfers between devices  8.88 us (24%)
  Pallas kernels  2.38 us (6%)
  matrix products  2.06 us (6%)
  local copies, waits for them, and re-layouts  1.97 us (5%)
  other arithmetic  1.09 us (3%)
    all_to_all x1, blocking collectives, per_device(): lax.all_to_all(computed.reshape(groups, capacity, feat), 'row', split_axi...  11.6 us
    all_to_all x1, starting transfers between devices, per_device(): lax.all_to_all(outgoing.reshape(groups, capacity, feat + 128), 'row', spl...  8.31 us
    all_to_all x1, waiting for transfers between devices, per_device(): lax.all_to_all(outgoing.reshape(groups, capacity, feat + 128), 'row', spl...  8.14 us
    pallas_call x1, Pallas kernels, apply_owner(): pl.pallas_call(owner_kernel, out_shape=jax.ShapeDtypeStruct((slots, field...  2.38 us
    unnamed x8, local copies, waits for them, and re-layouts  1.88 us
    dot_general x1, matrix products, per_device(): jnp.dot(pack, air_ext, preferred_element_type=jnp.float32)  0.91 us
    dot_general x1, matrix products, per_device(): lax.dot_general(pack, returned, (((0,), (0,)), ((), ())), preferred_eleme...  0.87 us
  transfers between devices with their start and end apart: 3, of which 3 were waited for; matrix products, arithmetic and copies ran while one was open for 1% of the time, Pallas kernels for 0%

profile of v3, /device:TPU:0, one launch (start us, length us, event | category | flops | bytes accessed | tf_op | source)
XLA Modules:
  0.0 37.0 jit_solution(8107767053129386396)
XLA Ops:
  0.0 0.7 %convert_element_type.30 = bf16[128]{0:T(256)(128)(2,1)S(1)} convert(s32[128]{0:T(128)} %param.7) | non-fusion elementwise | flops 128 | bytes 768 | tf_op jit(solution)/shard_map/convert_element_type | solution.py:95
  0.7 0.0 copy-start.2
  0.7 0.7 %copy-done.2 = s32[128,1]{0,1:T(1,128)S(1)} copy-done((s32[128,1]{0,1:T(1,128)S(1)}, s32[128,1]{0,1:T(1,128)}, u32[]{:S(2)}) %copy-start.2) | copy-done | bytes 536
  1.3 0.1 fusion.20
  1.4 0.0 copy-start.1
  1.4 0.2 reduce_window_sum.11
  1.6 0.2 select_reduce_fusion
  1.8 0.1 broadcast_in_dim.2
  1.9 0.4 %copy-done.1 = bf16[128,384]{1,0:T(8,128)(2,1)S(1)} copy-done((bf16[128,384]{1,0:T(8,128)(2,1)S(1)}, bf16[128,384]{1,0:T(8,128)(2,1)}, u32[]{:S(2)}) %copy-start.1) | copy-done | bytes 98328
  2.3 0.9 %convolution_convert_fusion = bf16[256,512]{1,0:T(8,128)(2,1)} fusion(bf16[128,128]{1,0:T(8,128)(2,1)S(1)} %broadcast_in_dim.2, bf16[128,384]{1,0:T(8,128)(2,1)S(1)} %copy-done.1, s32[128]{0:T(128)S(1)} %multiply_add_fusion), kind=kOutput, calls=%fused_computation | convolution fusion | flops 33980416 | bytes 393728 | tf_op jit(solution)/shard_map/dot_general | solution.py:97
  3.2 8.3 %all-to-all-start = ((bf16[16,16,512]{2,1,0:T(8,128)(2,1)}), bf16[16,16,512]{2,1,0:T(8,128)(2,1)S(1)}, u32[]{:S(2)}, u32[]{:S(2)}) async-start(bf16[16,16,512]{2,1,0:T(8,128)(2,1)} %bitcast.1), calls=%async_computation | async-start | bytes 524288 | tf_op jit(solution)/shard_map/all_to_all | solution.py:98
  11.5 0.0 copy-start.3
  11.6 0.1 collective-permute-start.1
  11.6 0.5 %collective-permute-start = (bf16[32,384]{1,0:T(8,128)(2,1)S(1)}, bf16[32,384]{1,0:T(8,128)(2,1)S(1)}, u32[]{:S(2)}, u32[]{:S(2)}) collective-permute-start(bf16[32,384]{1,0:T(8,128)(2,1)S(1)} %get-tuple-element.9), channel_id=1, source_target_pairs={{0,1},{1,0},{2,3},{3,2},{4,5},{5,4},{6,7},{7,6},{8,9},{9,8},{10,11... | collective-permute-start | bytes 73736 | tf_op jit(solution)/shard_map/ppermute | solution.py:17
  12.1 0.1 copy-done.3
  12.2 0.6 %collective-permute-done.1 = bf16[32,384]{1,0:T(8,128)(2,1)S(1)} collective-permute-done((bf16[32,384]{1,0:T(8,128)(2,1)S(1)}, bf16[32,384]{1,0:T(8,128)(2,1)S(1)}, u32[]{:S(2)}, u32[]{:S(2)}) %collective-permute-start.1) | collective-permute-done | bytes 24608 | tf_op jit(solution)/shard_map/ppermute | solution.py:19
  12.8 0.2 collective-permute-done
  13.0 0.3 fusion.1
  13.3 8.1 %all-to-all-done = bf16[16,16,512]{2,1,0:T(8,128)(2,1)S(1)} async-done(((bf16[16,16,512]{2,1,0:T(8,128)(2,1)}), bf16[16,16,512]{2,1,0:T(8,128)(2,1)S(1)}, u32[]{:S(2)}, u32[]{:S(2)}) %all-to-all-start) | async-done | bytes 262176 | tf_op jit(solution)/shard_map/all_to_all | solution.py:98
  21.4 0.0 copy-start
  21.4 0.7 %copy-done = bf16[16,16,512]{2,1,0:T(8,128)(2,1)} copy-done((bf16[16,16,512]{2,1,0:T(8,128)(2,1)}, bf16[16,16,512]{2,1,0:T(8,128)(2,1)S(1)}, u32[]{:S(2)}) %copy-start) | copy-done | bytes 262168
  22.1 2.4 %shard_map.55 = bf16[256,384]{1,0:T(8,128)(2,1)} custom-call(bf16[256,512]{1,0:T(8,128)(2,1)} %bitcast.16, bf16[4,3,128,128]{3,2,1,0:T(8,128)(2,1)} %bitcast.19), custom_call_target="tpu_custom_call" | custom-call | flops 100663296 | bytes 851968 | tf_op jit(solution)/shard_map/pallas_call | solution.py:61
  24.5 11.6 %all_to_all.10 = bf16[16,16,384]{2,1,0:T(8,128)(2,1)S(1)} all-to-all(bf16[16,16,384]{2,1,0:T(8,128)(2,1)} %bitcast.18), channel_id=1, replica_groups=mesh['row'=16,'col'=2] {'row'}, dimensions={0} | all-to-all | bytes 393216 | tf_op jit(solution)/shard_map/all_to_all | solution.py:115
  36.1 0.9 %fusion = bf16[128,384]{1,0:T(8,128)(2,1)} fusion(f32[128,384]{1,0:T(8,128)S(1)} %fusion.1, bf16[256,384]{1,0:T(8,128)(2,1)S(1)} %bitcast.17, s32[128]{0:T(128)S(1)} %multiply_add_fusion), kind=kOutput, calls=%fused_computation.2 | convolution fusion | flops 25296896 | bytes 492032 | tf_op jit(solution)/shard_map/dot_general | solution.py:118
  (4 shorter events, 0.0 us)
Async XLA Ops:
  0.7 0.7 %copy-start.2 = (s32[128,1]{0,1:T(1,128)S(1)}, s32[128,1]{0,1:T(1,128)}, u32[]{:S(2)}) copy-start(s32[128,1]{0,1:T(1,128)} %param.6) | copy-start | bytes 1540
  1.4 0.9 %copy-start.1 = (bf16[128,384]{1,0:T(8,128)(2,1)S(1)}, bf16[128,384]{1,0:T(8,128)(2,1)}, u32[]{:S(2)}) copy-start(bf16[128,384]{1,0:T(8,128)(2,1)} %param.5) | copy-start | bytes 294916
  3.2 18.2 %all-to-all-start = ((bf16[16,16,512]{2,1,0:T(8,128)(2,1)}), bf16[16,16,512]{2,1,0:T(8,128)(2,1)S(1)}, u32[]{:S(2)}, u32[]{:S(2)}) async-start(bf16[16,16,512]{2,1,0:T(8,128)(2,1)} %bitcast.1), calls=%async_computation | async-start | bytes 524288 | tf_op jit(solution)/shard_map/all_to_all | solution.py:98
  11.5 0.7 %copy-start.3 = (s32[4,128]{1,0:T(4,128)S(1)}, s32[4,128]{1,0:T(4,128)}, u32[]{:S(2)}) copy-start(s32[4,128]{1,0:T(4,128)} %param.8) | copy-start | bytes 6148
  11.6 1.3 %collective-permute-start.1 = (bf16[32,384]{1,0:T(8,128)(2,1)S(1)}, bf16[32,384]{1,0:T(8,128)(2,1)S(1)}, u32[]{:S(2)}, u32[]{:S(2)}) collective-permute-start(bf16[32,384]{1,0:T(8,128)(2,1)S(1)} %get-tuple-element.10), channel_id=1, source_target_pairs={{1,0},{0,1},{3,2},{2,3},{5,4},{4,5},{7,6},{6,7},{9,8},{8,9},{11,10... | collective-permute-start | bytes 73736 | tf_op jit(solution)/shard_map/ppermute | solution.py:19
  11.6 1.3 %collective-permute-start = (bf16[32,384]{1,0:T(8,128)(2,1)S(1)}, bf16[32,384]{1,0:T(8,128)(2,1)S(1)}, u32[]{:S(2)}, u32[]{:S(2)}) collective-permute-start(bf16[32,384]{1,0:T(8,128)(2,1)S(1)} %get-tuple-element.9), channel_id=1, source_target_pairs={{0,1},{1,0},{2,3},{3,2},{4,5},{5,4},{6,7},{7,6},{8,9},{9,8},{10,11... | collective-permute-start | bytes 73736 | tf_op jit(solution)/shard_map/ppermute | solution.py:17
  21.4 0.7 %copy-start = (bf16[16,16,512]{2,1,0:T(8,128)(2,1)}, bf16[16,16,512]{2,1,0:T(8,128)(2,1)S(1)}, u32[]{:S(2)}) copy-start(bf16[16,16,512]{2,1,0:T(8,128)(2,1)S(1)} %all-to-all-done) | copy-start | bytes 786436

commit v4 on v2

--- a/solution.py
+++ b/solution.py
@@ -50,7 +50,10 @@
             transcendentals=0,
             bytes_accessed=2 * (received.size + own_blocks.size + slots * fields * levels),
         ),
-    )(received, own_blocks)
+    )(
+        pltpu.with_memory_space_constraint(received, pltpu.MemorySpace.VMEM),
+        pltpu.with_memory_space_constraint(own_blocks, pltpu.MemorySpace.VMEM),
+    )
 
 
 def per_device(air_state, owner_map, cost_class, connectivity, inverse_blocks):

time: 35.5 us -> 34.2 us (0.963)
  Pallas kernels: 2.12 us -> 1.04 us
    pallas_call x1, Pallas kernels: 2.12 us -> 1.04 us  [apply_owner(): pl.pallas_call(owner_kernel, out_shape=jax.ShapeDtypeStruct((slots, field...]
    unnamed x8 -> x10, local copies, waits for them, and re-layouts: 1.41 us -> 1.41 us
where the time goes in v4:
time: 34.2 us; the launch traced here: 33.9 us
  blocking collectives  18 us (53%)
  waiting for transfers between devices  7.38 us (22%)
  starting transfers between devices  4.11 us (12%)
  local copies, waits for them, and re-layouts  1.5 us (4%)
  matrix products  1.37 us (4%)
  Pallas kernels  1.04 us (3%)
  other arithmetic  0.44 us (1%)
    all_to_all x1, blocking collectives, per_device(): lax.all_to_all(outgoing.reshape(groups, capacity, feat + 128), 'row', spl...  18 us
    all_to_all x1, waiting for transfers between devices, per_device(): lax.all_to_all(computed.reshape(groups, capacity, feat), 'row', split_axi...  7.37 us
    all_to_all x1, starting transfers between devices, per_device(): lax.all_to_all(computed.reshape(groups, capacity, feat), 'row', split_axi...  3.54 us
    unnamed x10, local copies, waits for them, and re-layouts  1.41 us
    pallas_call x1, Pallas kernels, apply_owner(): pl.pallas_call(owner_kernel, out_shape=jax.ShapeDtypeStruct((slots, field...  1.04 us
    dot_general x1, matrix products, per_device(): lap = jnp.dot(band, extended, preferred_element_type=jnp.float32)  0.92 us
  transfers between devices with their start and end apart: 3, of which 1 were waited for; matrix products, arithmetic and copies ran while one was open for 1% of the time, Pallas kernels for 0%

profile of v4, /device:TPU:0, one launch (start us, length us, event | category | flops | bytes accessed | tf_op | source)
XLA Modules:
  0.0 33.9 jit_solution(4792639444289736718)
XLA Ops:
  0.0 0.0 copy-start.2
  0.0 0.7 %copy-done.2 = s32[128,1]{0,1:T(1,128)S(1)} copy-done((s32[128,1]{0,1:T(1,128)S(1)}, s32[128,1]{0,1:T(1,128)}, u32[]{:S(2)}) %copy-start.2) | copy-done | bytes 536
  0.7 0.1 fusion.20
  0.7 0.0 copy-start.1
  0.8 0.2 reduce_window_sum.11
  0.9 0.2 select_reduce_fusion
  1.1 0.0 copy-start.4
  1.1 0.6 %copy-done.4 = s32[128]{0:T(128)S(1)} copy-done((s32[128]{0:T(128)S(1)}, s32[128]{0:T(128)}, u32[]{:S(2)}) %copy-start.4) | copy-done | bytes 536
  1.8 0.1 broadcast_in_dim.2
  1.9 0.0 copy-done.1
  1.9 0.0 copy-start
  1.9 0.2 convolution_convert_fusion
  2.1 18.0 %all_to_all.10 = bf16[16,16,512]{2,1,0:T(8,128)(2,1)S(1)} all-to-all(bf16[16,16,512]{2,1,0:T(8,128)(2,1)S(1)} %bitcast.18), channel_id=1, replica_groups=mesh['row'=16,'col'=2] {'row'}, dimensions={0} | all-to-all | bytes 524288 | tf_op jit(solution)/shard_map/all_to_all | solution.py:77
  20.1 0.0 copy-done
  20.1 1.0 %shard_map.55 = bf16[256,384]{1,0:T(8,128)(2,1)} custom-call(bf16[256,512]{1,0:T(8,128)(2,1)S(1)} %bitcast.16, bf16[4,3,128,128]{3,2,1,0:T(8,128)(2,1)S(1)} %bitcast.17), custom_call_target="tpu_custom_call" | custom-call | flops 100663296 | bytes 851968 | tf_op jit(solution)/shard_map/pallas_call | solution.py:43
  21.1 3.5 %all-to-all-start.1 = ((bf16[16,16,384]{2,1,0:T(8,128)(2,1)}), bf16[16,16,384]{2,1,0:T(8,128)(2,1)S(1)}, u32[]{:S(2)}, u32[]{:S(2)}) async-start(bf16[16,16,384]{2,1,0:T(8,128)(2,1)} %bitcast.20), calls=%async_computation.1 | async-start | bytes 393216 | tf_op jit(solution)/shard_map/all_to_all | solution.py:93
  24.7 0.0 copy-start.3
  24.7 0.1 collective-permute-start
  24.8 0.5 %collective-permute-start.1 = (bf16[32,384]{1,0:T(8,128)(2,1)S(1)}, bf16[32,384]{1,0:T(8,128)(2,1)S(1)}, u32[]{:S(2)}, u32[]{:S(2)}) collective-permute-start(bf16[32,384]{1,0:T(8,128)(2,1)S(1)} %get-tuple-element.6), channel_id=1, source_target_pairs={{1,0},{0,1},{3,2},{2,3},{5,4},{4,5},{7,6},{6,7},{9,8},{8,9},{11,10... | collective-permute-start | bytes 73736 | tf_op jit(solution)/shard_map/ppermute | solution.py:19
  25.3 0.1 copy-done.3
  25.4 7.4 %all-to-all-done.1 = bf16[16,16,384]{2,1,0:T(8,128)(2,1)S(1)} async-done(((bf16[16,16,384]{2,1,0:T(8,128)(2,1)}), bf16[16,16,384]{2,1,0:T(8,128)(2,1)S(1)}, u32[]{:S(2)}, u32[]{:S(2)}) %all-to-all-start.1) | async-done | bytes 196640 | tf_op jit(solution)/shard_map/all_to_all | solution.py:93
  32.8 0.2 fusion.9
  33.0 0.0 collective-permute-done
  33.0 0.0 collective-permute-done.1
  33.0 0.9 %fusion = bf16[128,384]{1,0:T(8,128)(2,1)} fusion(f32[128,384]{1,0:T(8,128)S(1)} %fusion.9, bf16[32,384]{1,0:T(8,128)(2,1)S(1)} %collective-permute-done.1, bf16[128,384]{1,0:T(8,128)(2,1)S(1)} %copy-done.1, bf16[32,384]{1,0:T(8,128)(2,1)S(1)} %collective-permute-done, s32[128]{0:T(128)S(1)} %get-tuple-element.11, s32[128]{0:T(128)S(1)} %get-tuple-element.9, ...), kind=kOutput, calls=%fused_computation.2 | convolution fusion | flops 19808256 | bytes 444928 | tf_op jit(solution)/shard_map/dot_general | solution.py:90
  (4 shorter events, 0.0 us)
Async XLA Ops:
  0.0 0.7 %copy-start.2 = (s32[128,1]{0,1:T(1,128)S(1)}, s32[128,1]{0,1:T(1,128)}, u32[]{:S(2)}) copy-start(s32[128,1]{0,1:T(1,128)} %param.6) | copy-start | bytes 1540
  0.7 1.1 %copy-start.1 = (bf16[128,384]{1,0:T(8,128)(2,1)S(1)}, bf16[128,384]{1,0:T(8,128)(2,1)}, u32[]{:S(2)}) copy-start(bf16[128,384]{1,0:T(8,128)(2,1)} %param.5) | copy-start | bytes 294916
  1.1 0.7 %copy-start.4 = (s32[128]{0:T(128)S(1)}, s32[128]{0:T(128)}, u32[]{:S(2)}) copy-start(s32[128]{0:T(128)} %param.7) | copy-start | bytes 1540
  1.9 18.2 %copy-start = (bf16[1,4,3,128,128]{4,3,2,1,0:T(8,128)(2,1)S(1)}, bf16[1,4,3,128,128]{4,3,2,1,0:T(8,128)(2,1)}, u32[]{:S(2)}) copy-start(bf16[1,4,3,128,128]{4,3,2,1,0:T(8,128)(2,1)} %param.9) | copy-start | bytes 1179652
  21.1 11.6 %all-to-all-start.1 = ((bf16[16,16,384]{2,1,0:T(8,128)(2,1)}), bf16[16,16,384]{2,1,0:T(8,128)(2,1)S(1)}, u32[]{:S(2)}, u32[]{:S(2)}) async-start(bf16[16,16,384]{2,1,0:T(8,128)(2,1)} %bitcast.20), calls=%async_computation.1 | async-start | bytes 393216 | tf_op jit(solution)/shard_map/all_to_all | solution.py:93
  24.7 0.7 %copy-start.3 = (s32[4,128]{1,0:T(4,128)S(1)}, s32[4,128]{1,0:T(4,128)}, u32[]{:S(2)}) copy-start(s32[4,128]{1,0:T(4,128)} %param.8) | copy-start | bytes 6148
  24.7 8.3 %collective-permute-start = (bf16[32,384]{1,0:T(8,128)(2,1)S(1)}, bf16[32,384]{1,0:T(8,128)(2,1)S(1)}, u32[]{:S(2)}, u32[]{:S(2)}) collective-permute-start(bf16[32,384]{1,0:T(8,128)(2,1)S(1)} %get-tuple-element.5), channel_id=1, source_target_pairs={{0,1},{1,0},{2,3},{3,2},{4,5},{5,4},{6,7},{7,6},{8,9},{9,8},{10,11... | collective-permute-start | bytes 73736 | tf_op jit(solution)/shard_map/ppermute | solution.py:17
  24.8 8.2 %collective-permute-start.1 = (bf16[32,384]{1,0:T(8,128)(2,1)S(1)}, bf16[32,384]{1,0:T(8,128)(2,1)S(1)}, u32[]{:S(2)}, u32[]{:S(2)}) collective-permute-start(bf16[32,384]{1,0:T(8,128)(2,1)S(1)} %get-tuple-element.6), channel_id=1, source_target_pairs={{1,0},{0,1},{3,2},{2,3},{5,4},{4,5},{7,6},{6,7},{9,8},{8,9},{11,10... | collective-permute-start | bytes 73736 | tf_op jit(solution)/shard_map/ppermute | solution.py:19

commit v5 on v4

--- a/solution.py
+++ b/solution.py
@@ -1,3 +1,5 @@
+import functools
+
 import jax
 import jax.numpy as jnp
 from jax import lax
@@ -19,6 +21,50 @@
             lax.ppermute(head, axis, [((i + 1) % count, i) for i in range(count)]),
         ],
         axis=0,
+    )
+
+
+def pack_kernel(capacity, air_ref, owner_ref, class_ref, out_ref, dest_ref):
+    count, feat = air_ref.shape
+    slots = out_ref.shape[0]
+    groups = slots // capacity
+    owner = owner_ref[...]
+    hits = (lax.broadcasted_iota(jnp.int32, (groups, count), 0) == owner).astype(jnp.float32)
+    earlier = (
+        lax.broadcasted_iota(jnp.int32, (count, count), 0)
+        <= lax.broadcasted_iota(jnp.int32, (count, count), 1)
+    ).astype(jnp.bfloat16)
+    running = jnp.dot(hits.astype(jnp.bfloat16), earlier, preferred_element_type=jnp.float32)
+    rank = jnp.sum(running * hits, axis=0, keepdims=True) - 1.0
+    dest = owner * capacity + rank.astype(jnp.int32)
+    dest_ref[...] = dest
+    chosen = lax.broadcasted_iota(jnp.int32, (slots, count), 0) == dest
+    moved = jnp.dot(chosen.astype(jnp.bfloat16), air_ref[...], preferred_element_type=jnp.float32)
+    label = jnp.sum(jnp.where(chosen, class_ref[...].astype(jnp.float32), 0.0), axis=1, keepdims=True)
+    out_ref[:, :feat] = moved.astype(out_ref.dtype)
+    out_ref[:, feat:] = jnp.broadcast_to(label, (slots, out_ref.shape[1] - feat)).astype(out_ref.dtype)
+
+
+def pack_columns(air_state, owner_row, class_row, capacity, slots):
+    count, feat = air_state.shape
+    vmem = pltpu.MemorySpace.VMEM
+    return pl.pallas_call(
+        functools.partial(pack_kernel, capacity),
+        out_shape=(
+            jax.ShapeDtypeStruct((slots, feat + 128), jnp.bfloat16),
+            jax.ShapeDtypeStruct((1, count), jnp.int32),
+        ),
+        in_specs=[pl.BlockSpec(memory_space=pltpu.VMEM)] * 3,
+        out_specs=(pl.BlockSpec(memory_space=pltpu.VMEM), pl.BlockSpec(memory_space=pltpu.VMEM)),
+        cost_estimate=pl.CostEstimate(
+            flops=2 * slots * count * feat + 2 * count * count * slots // capacity,
+            transcendentals=0,
+            bytes_accessed=2 * (air_state.size + slots * (feat + 128)) + 12 * count,
+        ),
+    )(
+        pltpu.with_memory_space_constraint(air_state, vmem),
+        pltpu.with_memory_space_constraint(owner_row, vmem),
+        pltpu.with_memory_space_constraint(class_row, vmem),
     )
 
 
@@ -65,15 +111,10 @@
     capacity = 2 * local_count // groups
     slots = groups * capacity
 
-    targets = owner_map[:, 0]
-    hits = (targets[:, None] == jnp.arange(groups, dtype=jnp.int32)[None, :]).astype(jnp.int32)
-    slot_index = jnp.sum((jnp.cumsum(hits, axis=0) - 1) * hits, axis=1)
-    dest = targets * capacity + slot_index
-    pack = (jnp.arange(slots, dtype=jnp.int32)[:, None] == dest[None, :]).astype(jnp.bfloat16)
-
-    label_lanes = jnp.broadcast_to(cost_class.astype(jnp.bfloat16)[:, None], (local_count, 128))
-    air_ext = jnp.concatenate([air_state, label_lanes], axis=1)
-    outgoing = jnp.dot(pack, air_ext, preferred_element_type=jnp.float32).astype(jnp.bfloat16)
+    outgoing, dest = pack_columns(
+        air_state, owner_map.reshape(1, local_count), cost_class.reshape(1, local_count), capacity, slots
+    )
+    pack = (jnp.arange(slots, dtype=jnp.int32)[:, None] == dest).astype(jnp.bfloat16)
     received = lax.all_to_all(
         outgoing.reshape(groups, capacity, feat + 128), "row", split_axis=0, concat_axis=0, tiled=True
     ).reshape(slots, feat + 128)

time: 34.2 us -> 36.6 us (1.070)
  local copies, waits for them, and re-layouts: 1.5 us -> 3.02 us
  Pallas kernels: 1.04 us -> 2.1 us
  other arithmetic: 0.44 us -> 0.01 us
    unnamed x10 -> x14, local copies, waits for them, and re-layouts: 1.41 us -> 3.02 us
    pallas_call x0 -> x1, Pallas kernels: none -> 1.04 us  [pack_columns(): pl.pallas_call(functools.partial(pack_kernel, capacity), out_shape=(jax.S...]
    ppermute x1, starting transfers between devices: 0.5 us -> 0.07 us  [padded(): lax.ppermute(head, axis, [((i + 1) % count, i) for i in range(count)])]
    ppermute x1, starting transfers between devices: 0.07 us -> 0.5 us  [padded(): lax.ppermute(tail, axis, [(i, (i + 1) % count) for i in range(count)])]
where the time goes in v5:
time: 36.6 us; the launch traced here: 36.1 us
  blocking collectives  18.2 us (50%)
  waiting for transfers between devices  7.37 us (20%)
  starting transfers between devices  4.24 us (12%)
  local copies, waits for them, and re-layouts  3.02 us (8%)
  Pallas kernels  2.1 us (6%)
  matrix products  1.15 us (3%)
    all_to_all x1, blocking collectives, per_device(): lax.all_to_all(outgoing.reshape(groups, capacity, feat + 128), 'row', spl...  18.2 us
    all_to_all x1, waiting for transfers between devices, per_device(): lax.all_to_all(computed.reshape(groups, capacity, feat), 'row', split_axi...  7.36 us
    all_to_all x1, starting transfers between devices, per_device(): lax.all_to_all(computed.reshape(groups, capacity, feat), 'row', split_axi...  3.67 us
    unnamed x14, local copies, waits for them, and re-layouts  3.02 us
    pallas_call x1, Pallas kernels, apply_owner(): pl.pallas_call(owner_kernel, out_shape=jax.ShapeDtypeStruct((slots, field...  1.05 us
    pallas_call x1, Pallas kernels, pack_columns(): pl.pallas_call(functools.partial(pack_kernel, capacity), out_shape=(jax.S...  1.04 us
    dot_general x1, matrix products, per_device(): lap = jnp.dot(band, extended, preferred_element_type=jnp.float32)  0.93 us
  transfers between devices with their start and end apart: 3, of which 1 were waited for; matrix products, arithmetic and copies ran while one was open for 1% of the time, Pallas kernels for 0%

profile of v5, /device:TPU:0, one launch (start us, length us, event | category | flops | bytes accessed | tf_op | source)
XLA Modules:
  0.0 36.1 jit_solution(7569932809055259582)
XLA Ops:
  0.0 0.0 copy-start
  0.0 0.0 copy-start.1
  0.0 0.9 %copy-done.1 = bf16[128,384]{1,0:T(8,128)(2,1)S(1)} copy-done((bf16[128,384]{1,0:T(8,128)(2,1)S(1)}, bf16[128,384]{1,0:T(8,128)(2,1)}, u32[]{:S(2)}) %copy-start.1) | copy-done | bytes 98328
  0.9 0.0 copy-start.3
  0.9 0.7 %copy-done.3 = s32[128,1]{0,1:T(1,128)S(1)} copy-done((s32[128,1]{0,1:T(1,128)S(1)}, s32[128,1]{0,1:T(1,128)}, u32[]{:S(2)}) %copy-start.3) | copy-done | bytes 536
  1.6 0.0 copy-start.4
  1.6 0.7 %copy-done.4 = s32[128]{0:T(128)S(1)} copy-done((s32[128]{0:T(128)S(1)}, s32[128]{0:T(128)}, u32[]{:S(2)}) %copy-start.4) | copy-done | bytes 536
  2.3 1.0 %shard_map.55 = (bf16[256,512]{1,0:T(8,128)(2,1)}, s32[1,128]{1,0:T(1,128)}) custom-call(bf16[128,384]{1,0:T(8,128)(2,1)S(1)} %copy-done.1, s32[1,128]{1,0:T(1,128)S(1)} %bitcast.19, s32[1,128]{1,0:T(1,128)S(1)} %bitcast.20), custom_call_target="tpu_custom_call" | custom-call | flops 25690112 | bytes 361984 | tf_op jit(solution)/shard_map/pallas_call | solution.py:51
  3.3 18.2 %all_to_all.10 = bf16[16,16,512]{2,1,0:T(8,128)(2,1)S(1)} all-to-all(bf16[16,16,512]{2,1,0:T(8,128)(2,1)} %bitcast.23), channel_id=1, replica_groups=mesh['row'=16,'col'=2] {'row'}, dimensions={0} | all-to-all | bytes 524288 | tf_op jit(solution)/shard_map/all_to_all | solution.py:118
  21.5 0.0 copy-done
  21.5 1.1 %shard_map.56 = bf16[256,384]{1,0:T(8,128)(2,1)} custom-call(bf16[256,512]{1,0:T(8,128)(2,1)S(1)} %bitcast.17, bf16[4,3,128,128]{3,2,1,0:T(8,128)(2,1)S(1)} %bitcast.18), custom_call_target="tpu_custom_call" | custom-call | flops 100663296 | bytes 851968 | tf_op jit(solution)/shard_map/pallas_call | solution.py:89
  22.5 0.0 copy-start.2
  22.5 3.7 %all-to-all-start.1 = ((bf16[16,16,384]{2,1,0:T(8,128)(2,1)}), bf16[16,16,384]{2,1,0:T(8,128)(2,1)S(1)}, u32[]{:S(2)}, u32[]{:S(2)}) async-start(bf16[16,16,384]{2,1,0:T(8,128)(2,1)} %bitcast.22), calls=%async_computation.1 | async-start | bytes 393216 | tf_op jit(solution)/shard_map/all_to_all | solution.py:134
  26.2 0.0 copy-done.2
  26.2 0.0 copy-start.5
  26.3 0.1 collective-permute-start.1
  26.3 0.5 %collective-permute-start = (bf16[32,384]{1,0:T(8,128)(2,1)S(1)}, bf16[32,384]{1,0:T(8,128)(2,1)S(1)}, u32[]{:S(2)}, u32[]{:S(2)}) collective-permute-start(bf16[32,384]{1,0:T(8,128)(2,1)S(1)} %get-tuple-element.9), channel_id=1, source_target_pairs={{0,1},{1,0},{2,3},{3,2},{4,5},{5,4},{6,7},{7,6},{8,9},{9,8},{10,11... | collective-permute-start | bytes 73736 | tf_op jit(solution)/shard_map/ppermute | solution.py:19
  26.8 0.1 copy-done.5
  26.9 7.4 %all-to-all-done.1 = bf16[16,16,384]{2,1,0:T(8,128)(2,1)S(1)} async-done(((bf16[16,16,384]{2,1,0:T(8,128)(2,1)}), bf16[16,16,384]{2,1,0:T(8,128)(2,1)S(1)}, u32[]{:S(2)}, u32[]{:S(2)}) %all-to-all-start.1) | async-done | bytes 196640 | tf_op jit(solution)/shard_map/all_to_all | solution.py:134
  34.3 0.0 copy-start.6
  34.3 0.7 %copy-done.6 = s32[1,128]{1,0:T(1,128)S(1)} copy-done((s32[1,128]{1,0:T(1,128)S(1)}, s32[1,128]{1,0:T(1,128)}, u32[]{:S(2)}) %copy-start.6) | copy-done | bytes 536
  35.0 0.2 fusion.6
  35.2 0.0 collective-permute-done.1
  35.2 0.0 collective-permute-done
  35.2 0.9 %fusion = bf16[128,384]{1,0:T(8,128)(2,1)} fusion(f32[128,384]{1,0:T(8,128)S(1)} %fusion.6, bf16[32,384]{1,0:T(8,128)(2,1)S(1)} %collective-permute-done.1, bf16[128,384]{1,0:T(8,128)(2,1)S(1)} %copy-done.2, bf16[32,384]{1,0:T(8,128)(2,1)S(1)} %collective-permute-done, s32[128]{0:T(128)S(1)} %get-tuple-element.15, s32[128]{0:T(128)S(1)} %get-tuple-element.13, ...), kind=kOutput, calls=%fused_computation.1 | convolution fusion | flops 19808256 | bytes 444928 | tf_op jit(solution)/shard_map/dot_general | solution.py:131
  (2 shorter events, 0.0 us)
Async XLA Ops:
  0.0 21.5 %copy-start = (bf16[1,4,3,128,128]{4,3,2,1,0:T(8,128)(2,1)S(1)}, bf16[1,4,3,128,128]{4,3,2,1,0:T(8,128)(2,1)}, u32[]{:S(2)}) copy-start(bf16[1,4,3,128,128]{4,3,2,1,0:T(8,128)(2,1)} %param.9) | copy-start | bytes 1179652
  0.0 0.9 %copy-start.1 = (bf16[128,384]{1,0:T(8,128)(2,1)S(1)}, bf16[128,384]{1,0:T(8,128)(2,1)}, u32[]{:S(2)}) copy-start(bf16[128,384]{1,0:T(8,128)(2,1)} %air_ref.1) | copy-start | bytes 294916
  0.9 0.7 %copy-start.3 = (s32[128,1]{0,1:T(1,128)S(1)}, s32[128,1]{0,1:T(1,128)}, u32[]{:S(2)}) copy-start(s32[128,1]{0,1:T(1,128)} %param.6) | copy-start | bytes 1540
  1.6 0.7 %copy-start.4 = (s32[128]{0:T(128)S(1)}, s32[128]{0:T(128)}, u32[]{:S(2)}) copy-start(s32[128]{0:T(128)} %param.7) | copy-start | bytes 1540
  22.5 3.7 %copy-start.2 = (bf16[128,384]{1,0:T(8,128)(2,1)S(1)}, bf16[128,384]{1,0:T(8,128)(2,1)}, u32[]{:S(2)}) copy-start(bf16[128,384]{1,0:T(8,128)(2,1)} %air_ref.1) | copy-start | bytes 294916
  22.5 11.8 %all-to-all-start.1 = ((bf16[16,16,384]{2,1,0:T(8,128)(2,1)}), bf16[16,16,384]{2,1,0:T(8,128)(2,1)S(1)}, u32[]{:S(2)}, u32[]{:S(2)}) async-start(bf16[16,16,384]{2,1,0:T(8,128)(2,1)} %bitcast.22), calls=%async_computation.1 | async-start | bytes 393216 | tf_op jit(solution)/shard_map/all_to_all | solution.py:134
  26.2 0.7 %copy-start.5 = (s32[4,128]{1,0:T(4,128)S(1)}, s32[4,128]{1,0:T(4,128)}, u32[]{:S(2)}) copy-start(s32[4,128]{1,0:T(4,128)} %param.8) | copy-start | bytes 6148
  26.3 8.9 %collective-permute-start.1 = (bf16[32,384]{1,0:T(8,128)(2,1)S(1)}, bf16[32,384]{1,0:T(8,128)(2,1)S(1)}, u32[]{:S(2)}, u32[]{:S(2)}) collective-permute-start(bf16[32,384]{1,0:T(8,128)(2,1)S(1)} %get-tuple-element.10), channel_id=1, source_target_pairs={{1,0},{0,1},{3,2},{2,3},{5,4},{4,5},{7,6},{6,7},{9,8},{8,9},{11,10... | collective-permute-start | bytes 73736 | tf_op jit(solution)/shard_map/ppermute | solution.py:21
  26.3 8.9 %collective-permute-start = (bf16[32,384]{1,0:T(8,128)(2,1)S(1)}, bf16[32,384]{1,0:T(8,128)(2,1)S(1)}, u32[]{:S(2)}, u32[]{:S(2)}) collective-permute-start(bf16[32,384]{1,0:T(8,128)(2,1)S(1)} %get-tuple-element.9), channel_id=1, source_target_pairs={{0,1},{1,0},{2,3},{3,2},{4,5},{5,4},{6,7},{7,6},{8,9},{9,8},{10,11... | collective-permute-start | bytes 73736 | tf_op jit(solution)/shard_map/ppermute | solution.py:19
  34.3 0.7 %copy-start.6 = (s32[1,128]{1,0:T(1,128)S(1)}, s32[1,128]{1,0:T(1,128)}, u32[]{:S(2)}) copy-start(s32[1,128]{1,0:T(1,128)} %get-tuple-element.7) | copy-start | bytes 1540

commit v6 on v4

--- a/solution.py
+++ b/solution.py
@@ -65,13 +65,15 @@
     capacity = 2 * local_count // groups
     slots = groups * capacity
 
-    targets = owner_map[:, 0]
+    combined = owner_map[:, 0] * classes + cost_class
+    targets = combined // classes
+    column_class = combined - targets * classes
     hits = (targets[:, None] == jnp.arange(groups, dtype=jnp.int32)[None, :]).astype(jnp.int32)
     slot_index = jnp.sum((jnp.cumsum(hits, axis=0) - 1) * hits, axis=1)
     dest = targets * capacity + slot_index
     pack = (jnp.arange(slots, dtype=jnp.int32)[:, None] == dest[None, :]).astype(jnp.bfloat16)
 
-    label_lanes = jnp.broadcast_to(cost_class.astype(jnp.bfloat16)[:, None], (local_count, 128))
+    label_lanes = jnp.broadcast_to(column_class.astype(jnp.bfloat16)[:, None], (local_count, 128))
     air_ext = jnp.concatenate([air_state, label_lanes], axis=1)
     outgoing = jnp.dot(pack, air_ext, preferred_element_type=jnp.float32).astype(jnp.bfloat16)
     received = lax.all_to_all(

time: 34.2 us -> 34.1 us (level)
  local copies, waits for them, and re-layouts: 1.5 us -> 0.63 us
  other arithmetic: 0.44 us -> 1.12 us
    unnamed x10 -> x6, local copies, waits for them, and re-layouts: 1.41 us -> 0.54 us
    convert_element_type x1, other arithmetic: 0.01 us -> 0.69 us  [per_device(): column_class.astype(jnp.bfloat16)[:, None]]
where the time goes in v6:
time: 34.1 us; the launch traced here: 33.7 us
  blocking collectives  18 us (53%)
  waiting for transfers between devices  7.38 us (22%)
  starting transfers between devices  4.11 us (12%)
  matrix products  1.37 us (4%)
  other arithmetic  1.12 us (3%)
  Pallas kernels  1.04 us (3%)
  local copies, waits for them, and re-layouts  0.63 us (2%)
    all_to_all x1, blocking collectives, per_device(): lax.all_to_all(outgoing.reshape(groups, capacity, feat + 128), 'row', spl...  18 us
    all_to_all x1, waiting for transfers between devices, per_device(): lax.all_to_all(computed.reshape(groups, capacity, feat), 'row', split_axi...  7.37 us
    all_to_all x1, starting transfers between devices, per_device(): lax.all_to_all(computed.reshape(groups, capacity, feat), 'row', split_axi...  3.54 us
    pallas_call x1, Pallas kernels, apply_owner(): pl.pallas_call(owner_kernel, out_shape=jax.ShapeDtypeStruct((slots, field...  1.04 us
    dot_general x1, matrix products, per_device(): lap = jnp.dot(band, extended, preferred_element_type=jnp.float32)  0.92 us
    convert_element_type x1, other arithmetic, per_device(): column_class.astype(jnp.bfloat16)[:, None]  0.69 us
  transfers between devices with their start and end apart: 3, of which 1 were waited for; matrix products, arithmetic and copies ran while one was open for 1% of the time, Pallas kernels for 0%

profile of v6, /device:TPU:0, one launch (start us, length us, event | category | flops | bytes accessed | tf_op | source)
XLA Modules:
  0.0 33.7 jit_solution(1920738814426863519)
XLA Ops:
  0.0 0.7 %subtract_convert_fusion = (bf16[128]{0:T(256)(128)(2,1)S(1)}, s32[128]{0:T(128)S(1)}) fusion(s32[128]{0:T(128)} %param.7, s32[128,1]{0,1:T(1,128)} %param.6), kind=kLoop, calls=%fused_computation.42 | loop fusion | flops 2560 | bytes 1792 | tf_op jit(solution)/shard_map/convert_element_type | solution.py:76
  0.7 0.1 fusion.20
  0.8 0.0 copy-start.1
  0.8 0.2 reduce_window_sum.11
  1.0 0.2 select_reduce_fusion
  1.1 0.1 broadcast_in_dim.2
  1.2 0.4 %copy-done.1 = bf16[128,384]{1,0:T(8,128)(2,1)S(1)} copy-done((bf16[128,384]{1,0:T(8,128)(2,1)S(1)}, bf16[128,384]{1,0:T(8,128)(2,1)}, u32[]{:S(2)}) %copy-start.1) | copy-done | bytes 98328
  1.7 0.0 copy-start
  1.7 0.2 convolution_convert_fusion
  1.9 18.0 %all_to_all.10 = bf16[16,16,512]{2,1,0:T(8,128)(2,1)S(1)} all-to-all(bf16[16,16,512]{2,1,0:T(8,128)(2,1)S(1)} %bitcast.23), channel_id=1, replica_groups=mesh['row'=16,'col'=2] {'row'}, dimensions={0} | all-to-all | bytes 524288 | tf_op jit(solution)/shard_map/all_to_all | solution.py:79
  19.9 0.0 copy-done
  19.9 1.0 %shard_map.55 = bf16[256,384]{1,0:T(8,128)(2,1)} custom-call(bf16[256,512]{1,0:T(8,128)(2,1)S(1)} %bitcast.21, bf16[4,3,128,128]{3,2,1,0:T(8,128)(2,1)S(1)} %bitcast.22), custom_call_target="tpu_custom_call" | custom-call | flops 100663296 | bytes 851968 | tf_op jit(solution)/shard_map/pallas_call | solution.py:43
  20.9 3.5 %all-to-all-start.1 = ((bf16[16,16,384]{2,1,0:T(8,128)(2,1)}), bf16[16,16,384]{2,1,0:T(8,128)(2,1)S(1)}, u32[]{:S(2)}, u32[]{:S(2)}) async-start(bf16[16,16,384]{2,1,0:T(8,128)(2,1)} %bitcast.25), calls=%async_computation.1 | async-start | bytes 393216 | tf_op jit(solution)/shard_map/all_to_all | solution.py:95
  24.5 0.0 copy-start.2
  24.5 0.1 collective-permute-start
  24.6 0.5 %collective-permute-start.1 = (bf16[32,384]{1,0:T(8,128)(2,1)S(1)}, bf16[32,384]{1,0:T(8,128)(2,1)S(1)}, u32[]{:S(2)}, u32[]{:S(2)}) collective-permute-start(bf16[32,384]{1,0:T(8,128)(2,1)S(1)} %get-tuple-element.8), channel_id=1, source_target_pairs={{1,0},{0,1},{3,2},{2,3},{5,4},{4,5},{7,6},{6,7},{9,8},{8,9},{11,10... | collective-permute-start | bytes 73736 | tf_op jit(solution)/shard_map/ppermute | solution.py:19
  25.1 0.1 copy-done.2
  25.2 7.4 %all-to-all-done.1 = bf16[16,16,384]{2,1,0:T(8,128)(2,1)S(1)} async-done(((bf16[16,16,384]{2,1,0:T(8,128)(2,1)}), bf16[16,16,384]{2,1,0:T(8,128)(2,1)S(1)}, u32[]{:S(2)}, u32[]{:S(2)}) %all-to-all-start.1) | async-done | bytes 196640 | tf_op jit(solution)/shard_map/all_to_all | solution.py:95
  32.6 0.2 fusion.9
  32.8 0.0 collective-permute-done
  32.8 0.0 collective-permute-done.1
  32.8 0.9 %fusion = bf16[128,384]{1,0:T(8,128)(2,1)} fusion(f32[128,384]{1,0:T(8,128)S(1)} %fusion.9, bf16[32,384]{1,0:T(8,128)(2,1)S(1)} %collective-permute-done.1, bf16[128,384]{1,0:T(8,128)(2,1)S(1)} %copy-done.1, bf16[32,384]{1,0:T(8,128)(2,1)S(1)} %collective-permute-done, s32[128]{0:T(128)S(1)} %get-tuple-element.13, s32[128]{0:T(128)S(1)} %get-tuple-element.11, ...), kind=kOutput, calls=%fused_computation.2 | convolution fusion | flops 19808256 | bytes 444928 | tf_op jit(solution)/shard_map/dot_general | solution.py:92
  (3 shorter events, 0.0 us)
Async XLA Ops:
  0.8 0.9 %copy-start.1 = (bf16[128,384]{1,0:T(8,128)(2,1)S(1)}, bf16[128,384]{1,0:T(8,128)(2,1)}, u32[]{:S(2)}) copy-start(bf16[128,384]{1,0:T(8,128)(2,1)} %param.5) | copy-start | bytes 294916
  1.7 18.2 %copy-start = (bf16[1,4,3,128,128]{4,3,2,1,0:T(8,128)(2,1)S(1)}, bf16[1,4,3,128,128]{4,3,2,1,0:T(8,128)(2,1)}, u32[]{:S(2)}) copy-start(bf16[1,4,3,128,128]{4,3,2,1,0:T(8,128)(2,1)} %param.9) | copy-start | bytes 1179652
  20.9 11.6 %all-to-all-start.1 = ((bf16[16,16,384]{2,1,0:T(8,128)(2,1)}), bf16[16,16,384]{2,1,0:T(8,128)(2,1)S(1)}, u32[]{:S(2)}, u32[]{:S(2)}) async-start(bf16[16,16,384]{2,1,0:T(8,128)(2,1)} %bitcast.25), calls=%async_computation.1 | async-start | bytes 393216 | tf_op jit(solution)/shard_map/all_to_all | solution.py:95
  24.5 0.7 %copy-start.2 = (s32[4,128]{1,0:T(4,128)S(1)}, s32[4,128]{1,0:T(4,128)}, u32[]{:S(2)}) copy-start(s32[4,128]{1,0:T(4,128)} %param.8) | copy-start | bytes 6148
  24.5 8.3 %collective-permute-start = (bf16[32,384]{1,0:T(8,128)(2,1)S(1)}, bf16[32,384]{1,0:T(8,128)(2,1)S(1)}, u32[]{:S(2)}, u32[]{:S(2)}) collective-permute-start(bf16[32,384]{1,0:T(8,128)(2,1)S(1)} %get-tuple-element.7), channel_id=1, source_target_pairs={{0,1},{1,0},{2,3},{3,2},{4,5},{5,4},{6,7},{7,6},{8,9},{9,8},{10,11... | collective-permute-start | bytes 73736 | tf_op jit(solution)/shard_map/ppermute | solution.py:17
  24.6 8.2 %collective-permute-start.1 = (bf16[32,384]{1,0:T(8,128)(2,1)S(1)}, bf16[32,384]{1,0:T(8,128)(2,1)S(1)}, u32[]{:S(2)}, u32[]{:S(2)}) collective-permute-start(bf16[32,384]{1,0:T(8,128)(2,1)S(1)} %get-tuple-element.8), channel_id=1, source_target_pairs={{1,0},{0,1},{3,2},{2,3},{5,4},{4,5},{7,6},{6,7},{9,8},{8,9},{11,10... | collective-permute-start | bytes 73736 | tf_op jit(solution)/shard_map/ppermute | solution.py:19
